TPU v7x, 128 devices: a whole 4x4x4 slice. The times are simulated.
128 devices in a mesh: dp: 16 (over y, z), sub: 8 (over x, core).
Axes of the slice: x: 4, y: 4, z: 4, core: 2. Of those that a mesh axis runs over, the one named last changes fastest.
Arguments:
- attn_heads: bfloat16 [8192, 2048], P(('dp', 'sub')), may hold values from -6 to 6
- residual: bfloat16 [8192, 2048], P(('dp', 'sub')), may hold values from -6 to 6
- out_weight: bfloat16 [2048, 2048], replicated, may hold values from -0.125 to 0.125
- norm_gain: float32 [2048], replicated, may hold values from 0.1 to 1.9
- router_weight: bfloat16 [2048, 32], replicated, may hold values from -13.258252 to 13.258252
- expert_ids: int32 [8192, 8], P(('dp', 'sub')), may hold values from 0 to 31, as said below
- holders: int32 [32, 4], replicated, may hold values from 0 to 127, as said below
- slot_gate_up: bfloat16 [128, 2048, 2048], P(('dp', 'sub')), may hold values from -0.13258252 to 0.13258252, as said below
- slot_down: bfloat16 [128, 1024, 2048], P(('dp', 'sub')), may hold values from -1.5 to 1.5, as said below
- next_gain: float32 [2048], replicated, may hold values from 0.1 to 1.9
Outputs:
- new_stream: float32 [8192, 2048], P(('dp', 'sub'))
- next_normed: float32 [8192, 2048], P(('dp', 'sub'))
Inputs may be any that keep to these rules, and one draw needn't show every extreme that they name: `expert_ids`: each row names 8 distinct experts. Among the rows of one device (aligned blocks of 64 rows) no expert is named more than 32 times, and one expert, drawn from the seed, is named exactly 32 times in every such block. Every device index appears exactly once in the table: each expert has 4 holders. `slot_gate_up`: devices that hold the same expert hold equal values. `slot_down`: devices that hold the same expert hold equal values.
All inputs are finite; a program needn't handle non-finite values.
Results may differ from a plain program's by a relative error of at most 0.009.
Values may be sent and summed in bfloat16 or wider, within the bound.
No kernel may reach another device: no remote copies, remote signals or barrier semaphores. Data moves between devices by JAX's collectives and lax.ppermute only.
A program may use at most 128 MiB of HBM per device.

v0:
```python
import jax
import jax.numpy as jnp
from jax import lax
from jax.sharding import PartitionSpec as P


def rms_factor(widened):
    return lax.rsqrt(jnp.mean(widened * widened, -1, keepdims=True) + 1e-05)


def body(
    attn_heads,
    residual,
    out_weight,
    norm_gain,
    router_weight,
    expert_ids,
    holders,
    slot_gate_up,
    slot_down,
    next_gain,
):
    tok_count, top_count = expert_ids.shape
    expert_count, copy_count = holders.shape
    model_width = attn_heads.shape[1]
    hidden_width = slot_down.shape[1]
    device_count = lax.axis_size("dp") * lax.axis_size("sub")
    capacity = 2 * tok_count * top_count // expert_count
    per_slot = capacity // copy_count
    projected = jnp.dot(attn_heads, out_weight, preferred_element_type=jnp.float32)
    stream = residual.astype(jnp.float32) + projected
    normed = (stream * rms_factor(stream) * norm_gain).astype(jnp.bfloat16)
    logits = jnp.dot(normed, router_weight, preferred_element_type=jnp.float32)
    weights_all = jax.nn.softmax(logits, axis=-1)
    chosen = expert_ids[:, :, None] == jnp.arange(expert_count, dtype=jnp.int32)[None, None, :]
    picked = jnp.sum(jnp.where(chosen, weights_all[:, None, :], 0.0), -1)
    flat_chosen = chosen.reshape(tok_count * top_count, expert_count).astype(jnp.int32)
    before = jnp.cumsum(flat_chosen, 0) - flat_chosen
    order_rank = jnp.sum(before * flat_chosen, -1)
    copy_index = order_rank % copy_count
    slot_place = order_rank // copy_count
    table_index = expert_ids.reshape(-1) * copy_count + copy_index
    table_range = jnp.arange(expert_count * copy_count, dtype=jnp.int32)
    slot_index = jnp.sum(
        jnp.where(table_index[:, None] == table_range[None, :], holders.reshape(-1)[None, :], 0), -1
    )
    target = slot_index * per_slot + slot_place
    source_row = jnp.arange(tok_count * top_count, dtype=jnp.int32) // top_count
    sender = jnp.full((device_count * per_slot,), -1, jnp.int32).at[target].set(source_row)
    filled = sender >= 0
    outgoing = jnp.where(
        filled[:, None], normed[jnp.maximum(sender, 0)], jnp.zeros((), jnp.bfloat16)
    )
    outgoing = outgoing.reshape(device_count, per_slot, model_width)
    gate_up = slot_gate_up[0]
    down_proj = slot_down[0]
    packet = lax.all_to_all(outgoing, ("dp", "sub"), split_axis=0, concat_axis=0, tiled=True)
    flat_rows = packet.reshape(-1, model_width)
    both_rows = jnp.dot(flat_rows, gate_up, preferred_element_type=jnp.float32)
    hidden = (jax.nn.silu(both_rows[:, :hidden_width]) * both_rows[:, hidden_width:]).astype(
        jnp.bfloat16
    )
    answer = jnp.dot(hidden, down_proj, preferred_element_type=jnp.float32).astype(jnp.bfloat16)
    returned = lax.all_to_all(
        answer.reshape(packet.shape), ("dp", "sub"), split_axis=0, concat_axis=0, tiled=True
    )
    results = returned.reshape(device_count * per_slot, model_width)[target]
    results = results.reshape(tok_count, top_count, model_width).astype(jnp.float32)
    expert_sum = jnp.einsum("tk,tkd->td", picked, results)
    new_stream = stream + expert_sum
    next_normed = new_stream * rms_factor(new_stream) * next_gain
    return (new_stream, next_normed)


def solution(mesh):
    in_specs = (
        P(("dp", "sub"), None),
        P(("dp", "sub"), None),
        P(),
        P(),
        P(),
        P(("dp", "sub"), None),
        P(),
        P(("dp", "sub"), None, None),
        P(("dp", "sub"), None, None),
        P(),
    )
    out_specs = (P(("dp", "sub"), None), P(("dp", "sub"), None))
    return jax.shard_map(body, mesh=mesh, in_specs=in_specs, out_specs=out_specs, check_vma=False)
```

profile of v0, /device:TPU:1, one launch (start us, length us, event | category | flops | bytes accessed | tf_op | source)
XLA Modules:
  0.0 170.1 jit_solution(16012636116224533119)
XLA Ops:
  0.6 0.8 copy.21
  1.6 0.8 copy.24
  2.4 0.1 broadcast_in_dim.63
  2.5 1.2 reduce-window.6
  3.7 0.2 slice_reduce_fusion
  4.0 0.1 fusion.14
  4.1 0.2 select_reduce_fusion
  4.4 2.4 %scatter_custom_fusion = s32[1024]{0:T(1024)S(1)} fusion(s32[512]{0:T(512)S(1)} %bitcast.51, s32[512]{0:T(512)S(1)} %add_select_fusion, s32[]{:T(128)} %constant.60.clone.1), kind=kCustom, calls=%fused_computation.56 | custom fusion | bytes 4100 | tf_op jit(solution)/shard_map/scatter | solution.py:49
  6.9 5.1 %multiply_reduce_fusion.1 = (f32[64]{0:T(128)S(1)}, f32[64,2048]{1,0:T(8,128)S(1)}) fusion(bf16[64,2048]{1,0:T(8,128)(2,1)S(1)} %copy-done, bf16[2048,2048]{1,0:T(8,128)(2,1)} %param.12, bf16[64,2048]{1,0:T(8,128)(2,1)} %param.11), kind=kOutput, calls=%fused_computation.20 | convolution fusion | flops 537395136 | bytes 9437440 | tf_op jit(solution)/shard_map/dot_general | solution.py:30
  12.0 0.1 broadcast_in_dim.66
  12.1 0.1 multiply_convert_fusion
  12.2 6.0 %gather_fusion = bf16[1024,2048]{1,0:T(8,128)(2,1)} fusion(bf16[64,2048]{1,0:T(8,128)(2,1)S(1)} %multiply_convert_fusion, s32[1024]{0:T(1024)S(1)} %maximum_clamp_fusion), kind=kCustom, calls=%fused_computation | custom fusion | bytes 8392704 | tf_op jit(solution)/shard_map/gather | solution.py:52
  18.2 2.5 %bitcast_select_fusion = bf16[128,8,2048]{2,1,0:T(8,128)(2,1)S(1)} fusion(bf16[1024,2048]{1,0:T(8,128)(2,1)} %gather_fusion, pred[128,8]{1,0:T(8,128)(4,1)S(1)} %broadcast_in_dim.66), kind=kLoop, calls=%fused_computation.10 | loop fusion | flops 2097152 | bytes 8389632 | tf_op jit(solution)/shard_map/jit(_where)/select_n | solution.py:51
  20.8 64.2 %all_to_all.10 = bf16[128,8,2048]{2,1,0:T(8,128)(2,1)S(1)} all-to-all(bf16[128,8,2048]{2,1,0:T(8,128)(2,1)S(1)} %bitcast_select_fusion), channel_id=1, replica_groups=mesh['dp'=16,'sub'=8] {'dp','sub'}, dimensions={0} | all-to-all | bytes 8388608 | tf_op jit(solution)/shard_map/all_to_all | solution.py:57
  85.0 11.4 %fusion = f32[1024,2048]{1,0:T(8,128)S(1)} fusion(bf16[1,2048,2048]{2,1,0:T(8,128)(2,1)} %param.17, bf16[128,8,2048]{2,1,0:T(8,128)(2,1)S(1)} %all_to_all.10), kind=kOutput, calls=%fused_computation.3 | convolution fusion | flops 8589934592 | bytes 20971520 | tf_op jit(solution)/shard_map/dot_general | solution.py:59
  96.4 6.2 %convert_bitcast_fusion = bf16[128,8,2048]{2,1,0:T(8,128)(2,1)} fusion(bf16[1,1024,2048]{2,1,0:T(8,128)(2,1)S(1)} %copy-done.6, f32[1024,2048]{1,0:T(8,128)S(1)} %fusion), kind=kOutput, calls=%fused_computation.11 | convolution fusion | flops 4303355904 | bytes 16777216 | tf_op jit(solution)/shard_map/dot_general | solution.py:63
  102.6 5.7 %all-to-all-start.1 = ((bf16[128,8,2048]{2,1,0:T(8,128)(2,1)}), bf16[128,8,2048]{2,1,0:T(8,128)(2,1)}, u32[]{:S(2)}, u32[]{:S(2)}) async-start(bf16[128,8,2048]{2,1,0:T(8,128)(2,1)} %convert_bitcast_fusion), calls=%async_computation.1 | async-start | bytes 8388608 | tf_op jit(solution)/shard_map/all_to_all | solution.py:64
  108.3 0.2 fusion.26
  108.6 0.1 copy.25
  108.7 52.3 %all-to-all-done.1 = bf16[128,8,2048]{2,1,0:T(8,128)(2,1)} async-done(((bf16[128,8,2048]{2,1,0:T(8,128)(2,1)}), bf16[128,8,2048]{2,1,0:T(8,128)(2,1)}, u32[]{:S(2)}, u32[]{:S(2)}) %all-to-all-start.1) | async-done | bytes 4194336 | tf_op jit(solution)/shard_map/all_to_all | solution.py:64
  161.0 7.1 %gather_fusion.1 = bf16[512,2048]{1,0:T(8,128)(2,1)S(1)} fusion(bf16[1024,2048]{1,0:T(8,128)(2,1)} %bitcast.10, s32[1024]{0:T(1024)S(1)} %pad_clamp_fusion), kind=kCustom, calls=%fused_computation.1 | custom fusion | bytes 4196352 | tf_op jit(solution)/shard_map/gather | solution.py:67
  168.1 0.7 fusion.9
  168.8 0.3 multiply_reduce_fusion
  169.1 0.9 multiply_multiply_fusion
  (31 shorter events, 0.4 us)
Async XLA Ops:
  0.6 6.2 %copy-start = (bf16[64,2048]{1,0:T(8,128)(2,1)S(1)}, bf16[64,2048]{1,0:T(8,128)(2,1)}, u32[]{:S(2)}) copy-start(bf16[64,2048]{1,0:T(8,128)(2,1)} %param.10) | copy-start | bytes 786436
  6.9 5.2 %copy-start.4 = (f32[2048]{0:T(1024)S(1)}, f32[2048]{0:T(1024)}, u32[]{:S(2)}) copy-start(f32[2048]{0:T(1024)} %param.13) | copy-start | bytes 24580
  85.0 11.4 %copy-start.6 = (bf16[1,1024,2048]{2,1,0:T(8,128)(2,1)S(1)}, bf16[1,1024,2048]{2,1,0:T(8,128)(2,1)}, u32[]{:S(2)}) copy-start(bf16[1,1024,2048]{2,1,0:T(8,128)(2,1)} %param.18) | copy-start | bytes 12582916
  102.6 5.7 %copy-start.2 = (bf16[2048,32]{0,1:T(8,128)(2,1)S(1)}, bf16[2048,32]{0,1:T(8,128)(2,1)}, u32[]{:S(2)}) copy-start(bf16[2048,32]{0,1:T(8,128)(2,1)} %param.14) | copy-start | bytes 393220
  102.6 5.9 %copy-start.3 = (s32[64,8]{0,1:T(8,128)S(1)}, s32[64,8]{0,1:T(8,128)}, u32[]{:S(2)}) copy-start(s32[64,8]{0,1:T(8,128)} %param.15) | copy-start | bytes 6148
  102.6 58.4 %all-to-all-start.1 = ((bf16[128,8,2048]{2,1,0:T(8,128)(2,1)}), bf16[128,8,2048]{2,1,0:T(8,128)(2,1)}, u32[]{:S(2)}, u32[]{:S(2)}) async-start(bf16[128,8,2048]{2,1,0:T(8,128)(2,1)} %convert_bitcast_fusion), calls=%async_computation.1 | async-start | bytes 8388608 | tf_op jit(solution)/shard_map/all_to_all | solution.py:64
  168.1 1.0 copy-start.5
  169.1 1.0 copy-start.1
where the time goes:
time: 170 us
  blocking collectives  64.2 us (38%)
  waiting for transfers between devices  52.3 us (31%)
  matrix products  23.5 us (14%)
  local copies, waits for them, and re-layouts  17.9 us (11%)
  starting transfers between devices  5.65 us (3%)
  other arithmetic  5.61 us (3%)
    all_to_all x1, blocking collectives, body(): lax.all_to_all(outgoing, ('dp', 'sub'), split_axis=0, concat_axis=0, tile...  64.2 us
    all_to_all x1, waiting for transfers between devices, body(): lax.all_to_all(answer.reshape(packet.shape), ('dp', 'sub'), split_axis=0,...  52.3 us
    dot_general x1, matrix products, body(): both_rows = jnp.dot(flat_rows, gate_up, preferred_element_type=jnp.float32)  11.4 us
    gather x1, local copies, waits for them, and re-layouts, body(): results = returned.reshape(device_count * per_slot, model_width)[target]  7.13 us
    dot_general x1, matrix products, body(): jnp.dot(hidden, down_proj, preferred_element_type=jnp.float32)  6.15 us
    gather x1, local copies, waits for them, and re-layouts, body(): normed[jnp.maximum(sender, 0)]  6.02 us
    all_to_all x1, starting transfers between devices, body(): lax.all_to_all(answer.reshape(packet.shape), ('dp', 'sub'), split_axis=0,...  5.65 us
    dot_general x1, matrix products, body(): jnp.dot(attn_heads, out_weight, preferred_element_type=jnp.float32)  5.08 us
  transfers between devices with their start and end apart: 1, of which 1 were waited for; matrix products, arithmetic and copies ran while one was open for 0% of the time, Pallas kernels for 0%

commit v1 on v0

--- a/solution.py
+++ b/solution.py
@@ -27,6 +27,7 @@
     device_count = lax.axis_size("dp") * lax.axis_size("sub")
     capacity = 2 * tok_count * top_count // expert_count
     per_slot = capacity // copy_count
+    slot_count = device_count * per_slot
     projected = jnp.dot(attn_heads, out_weight, preferred_element_type=jnp.float32)
     stream = residual.astype(jnp.float32) + projected
     normed = (stream * rms_factor(stream) * norm_gain).astype(jnp.bfloat16)
@@ -45,12 +46,10 @@
         jnp.where(table_index[:, None] == table_range[None, :], holders.reshape(-1)[None, :], 0), -1
     )
     target = slot_index * per_slot + slot_place
-    source_row = jnp.arange(tok_count * top_count, dtype=jnp.int32) // top_count
-    sender = jnp.full((device_count * per_slot,), -1, jnp.int32).at[target].set(source_row)
-    filled = sender >= 0
-    outgoing = jnp.where(
-        filled[:, None], normed[jnp.maximum(sender, 0)], jnp.zeros((), jnp.bfloat16)
-    )
+    hits = target[None, :] == jnp.arange(slot_count, dtype=jnp.int32)[:, None]
+    hits = hits.reshape(slot_count, tok_count, top_count)
+    send_map = jnp.any(hits, -1).astype(jnp.bfloat16)
+    outgoing = jnp.dot(send_map, normed, preferred_element_type=jnp.float32).astype(jnp.bfloat16)
     outgoing = outgoing.reshape(device_count, per_slot, model_width)
     gate_up = slot_gate_up[0]
     down_proj = slot_down[0]
@@ -64,9 +63,13 @@
     returned = lax.all_to_all(
         answer.reshape(packet.shape), ("dp", "sub"), split_axis=0, concat_axis=0, tiled=True
     )
-    results = returned.reshape(device_count * per_slot, model_width)[target]
-    results = results.reshape(tok_count, top_count, model_width).astype(jnp.float32)
-    expert_sum = jnp.einsum("tk,tkd->td", picked, results)
+    returned = returned.reshape(slot_count, model_width)
+    mix = jnp.sum(jnp.where(hits, picked[None, :, :], 0.0), -1).T
+    mix_high = lax.reduce_precision(mix, exponent_bits=8, mantissa_bits=7)
+    mix_low = mix - mix_high
+    mix_both = jnp.concatenate([mix_high, mix_low], 0).astype(jnp.bfloat16)
+    summed = jnp.dot(mix_both, returned, preferred_element_type=jnp.float32)
+    expert_sum = summed[:tok_count] + summed[tok_count:]
     new_stream = stream + expert_sum
     next_normed = new_stream * rms_factor(new_stream) * next_gain
     return (new_stream, next_normed)

time: 170 us -> 156 us (0.918)
  local copies, waits for them, and re-layouts: 17.9 us -> 2.38 us
  matrix products: 23.5 us -> 27.1 us
    gather x2 -> x0, local copies, waits for them, and re-layouts: 13.2 us -> none  [the longest x1 7.13 us: body(): results = returned.reshape(device_count * per_slot, model_width)[target]]
    dot_general x1 -> x2, matrix products: 0.69 us -> 4.24 us  [the longest x1 2.91 us: body(): summed = jnp.dot(mix_both, returned, preferred_element_type=jnp.float32)]
    select_n x3 -> x0, other arithmetic: 2.57 us -> none  [the longest x1 2.55 us: body(): jnp.where(filled[:, None], normed[jnp.maximum(sender, 0)], jnp.zeros((),...]
    scatter x1 -> x0, local copies, waits for them, and re-layouts: 2.45 us -> none  [body(): jnp.full((device_count * per_slot,), -1, jnp.int32).at[target]]
  transfers between devices with their start and end apart: 1 -> 1, of which waited for: 1 -> 1; matrix products, arithmetic and copies ran while one was open for 0% -> 1% of each run, Pallas kernels for 0% -> 0%
where the time goes in v1:
time: 156 us
  blocking collectives  64.2 us (41%)
  waiting for transfers between devices  51.5 us (33%)
  matrix products  27.1 us (17%)
  starting transfers between devices  5.64 us (4%)
  other arithmetic  4.28 us (3%)
  local copies, waits for them, and re-layouts  2.38 us (2%)
    all_to_all x1, blocking collectives, body(): lax.all_to_all(outgoing, ('dp', 'sub'), split_axis=0, concat_axis=0, tile...  64.2 us
    all_to_all x1, waiting for transfers between devices, body(): lax.all_to_all(answer.reshape(packet.shape), ('dp', 'sub'), split_axis=0,...  51.5 us
    dot_general x1, matrix products, body(): both_rows = jnp.dot(flat_rows, gate_up, preferred_element_type=jnp.float32)  11.4 us
    dot_general x1, matrix products, body(): jnp.dot(hidden, down_proj, preferred_element_type=jnp.float32)  6.15 us
    all_to_all x1, starting transfers between devices, body(): lax.all_to_all(answer.reshape(packet.shape), ('dp', 'sub'), split_axis=0,...  5.64 us
    dot_general x1, matrix products, body(): jnp.dot(attn_heads, out_weight, preferred_element_type=jnp.float32)  5.08 us
  transfers between devices with their start and end apart: 1, of which 1 were waited for; matrix products, arithmetic and copies ran while one was open for 1% of the time, Pallas kernels for 0%

profile of v1, /device:TPU:1, one launch (start us, length us, event | category | flops | bytes accessed | tf_op | source)
XLA Modules:
  0.0 155.9 jit_solution(10919006178992338254)
XLA Ops:
  0.6 0.8 copy.21
  1.5 0.1 reshape.113
  1.6 0.1 eq.62
  1.7 1.2 reduce-window.6
  2.8 0.2 slice_reduce_fusion
  3.1 0.1 fusion.20
  3.2 0.1 reduce_sum.67
  3.3 0.8 copy.24
  4.1 0.1 broadcast_in_dim.52
  4.2 0.2 select_reduce_fusion.1
  4.4 0.1 mul.76
  4.5 0.7 fusion.12
  5.3 5.1 %multiply_reduce_fusion.1 = (f32[64]{0:T(128)S(1)}, f32[64,2048]{1,0:T(8,128)S(1)}) fusion(bf16[64,2048]{1,0:T(8,128)(2,1)S(1)} %copy-done, bf16[2048,2048]{1,0:T(8,128)(2,1)} %param.12, bf16[64,2048]{1,0:T(8,128)(2,1)} %param.11), kind=kOutput, calls=%fused_computation.21 | convolution fusion | flops 537395136 | bytes 9437440 | tf_op jit(solution)/shard_map/dot_general | solution.py:31
  10.4 1.3 convert_bitcast_fusion.1
  11.7 64.2 %all_to_all.10 = bf16[128,8,2048]{2,1,0:T(8,128)(2,1)S(1)} all-to-all(bf16[128,8,2048]{2,1,0:T(8,128)(2,1)S(1)} %convert_bitcast_fusion.1), channel_id=1, replica_groups=mesh['dp'=16,'sub'=8] {'dp','sub'}, dimensions={0} | all-to-all | bytes 8388608 | tf_op jit(solution)/shard_map/all_to_all | solution.py:56
  75.9 11.4 %fusion = f32[1024,2048]{1,0:T(8,128)S(1)} fusion(bf16[1,2048,2048]{2,1,0:T(8,128)(2,1)} %param.17, bf16[128,8,2048]{2,1,0:T(8,128)(2,1)S(1)} %all_to_all.10), kind=kOutput, calls=%fused_computation | convolution fusion | flops 8589934592 | bytes 20971520 | tf_op jit(solution)/shard_map/dot_general | solution.py:58
  87.3 6.2 %convert_bitcast_fusion = bf16[128,8,2048]{2,1,0:T(8,128)(2,1)} fusion(bf16[1,1024,2048]{2,1,0:T(8,128)(2,1)S(1)} %copy-done.6, f32[1024,2048]{1,0:T(8,128)S(1)} %fusion), kind=kOutput, calls=%fused_computation.9 | convolution fusion | flops 4303355904 | bytes 16777216 | tf_op jit(solution)/shard_map/dot_general | solution.py:62
  93.5 5.6 %all-to-all-start.1 = ((bf16[128,8,2048]{2,1,0:T(8,128)(2,1)}), bf16[128,8,2048]{2,1,0:T(8,128)(2,1)}, u32[]{:S(2)}, u32[]{:S(2)}) async-start(bf16[128,8,2048]{2,1,0:T(8,128)(2,1)} %convert_bitcast_fusion), calls=%async_computation.1 | async-start | bytes 8388608 | tf_op jit(solution)/shard_map/all_to_all | solution.py:63
  99.1 0.3 fusion.33
  99.6 0.7 select_reduce_fusion
  100.4 51.5 %all-to-all-done.1 = bf16[128,8,2048]{2,1,0:T(8,128)(2,1)} async-done(((bf16[128,8,2048]{2,1,0:T(8,128)(2,1)}), bf16[128,8,2048]{2,1,0:T(8,128)(2,1)}, u32[]{:S(2)}, u32[]{:S(2)}) %all-to-all-start.1) | async-done | bytes 4194336 | tf_op jit(solution)/shard_map/all_to_all | solution.py:63
  151.9 2.9 %fusion.3 = f32[128,2048]{1,0:T(8,128)S(1)} fusion(bf16[128,8,2048]{2,1,0:T(8,128)(2,1)} %all-to-all-done.1, bf16[64,1024]{1,0:T(8,128)(2,1)S(1)} %get-tuple-element.5, bf16[64,1024]{1,0:T(8,128)(2,1)S(1)} %get-tuple-element.4), kind=kOutput, calls=%fused_computation.4 | convolution fusion | flops 537395200 | bytes 5505024 | tf_op jit(solution)/shard_map/dot_general | solution.py:71
  154.8 0.2 multiply_reduce_fusion
  155.0 0.9 multiply_multiply_fusion
  (27 shorter events, 0.3 us)
Async XLA Ops:
  0.6 4.6 %copy-start = (bf16[64,2048]{1,0:T(8,128)(2,1)S(1)}, bf16[64,2048]{1,0:T(8,128)(2,1)}, u32[]{:S(2)}) copy-start(bf16[64,2048]{1,0:T(8,128)(2,1)} %param.10) | copy-start | bytes 786436
  5.3 5.1 %copy-start.3 = (f32[2048]{0:T(1024)S(1)}, f32[2048]{0:T(1024)}, u32[]{:S(2)}) copy-start(f32[2048]{0:T(1024)} %param.13) | copy-start | bytes 24580
  75.9 11.4 %copy-start.6 = (bf16[1,1024,2048]{2,1,0:T(8,128)(2,1)S(1)}, bf16[1,1024,2048]{2,1,0:T(8,128)(2,1)}, u32[]{:S(2)}) copy-start(bf16[1,1024,2048]{2,1,0:T(8,128)(2,1)} %param.18) | copy-start | bytes 12582916
  93.5 5.7 %copy-start.2 = (bf16[2048,32]{0,1:T(8,128)(2,1)S(1)}, bf16[2048,32]{0,1:T(8,128)(2,1)}, u32[]{:S(2)}) copy-start(bf16[2048,32]{0,1:T(8,128)(2,1)} %param.14) | copy-start | bytes 393220
  93.5 6.0 %copy-start.4 = (s32[64,8]{0,1:T(8,128)S(1)}, s32[64,8]{0,1:T(8,128)}, u32[]{:S(2)}) copy-start(s32[64,8]{0,1:T(8,128)} %param.15) | copy-start | bytes 6148
  93.5 58.4 %all-to-all-start.1 = ((bf16[128,8,2048]{2,1,0:T(8,128)(2,1)}), bf16[128,8,2048]{2,1,0:T(8,128)(2,1)}, u32[]{:S(2)}, u32[]{:S(2)}) async-start(bf16[128,8,2048]{2,1,0:T(8,128)(2,1)} %convert_bitcast_fusion), calls=%async_computation.1 | async-start | bytes 8388608 | tf_op jit(solution)/shard_map/all_to_all | solution.py:63
  99.6 55.4 %copy-start.5 = (f32[2048]{0:T(1024)S(1)}, f32[2048]{0:T(1024)}, u32[]{:S(2)}) copy-start(f32[2048]{0:T(1024)} %param.19) | copy-start | bytes 24580
  155.0 1.0 copy-start.1

commit v2 on v1

--- a/solution.py
+++ b/solution.py
@@ -35,9 +35,12 @@
     weights_all = jax.nn.softmax(logits, axis=-1)
     chosen = expert_ids[:, :, None] == jnp.arange(expert_count, dtype=jnp.int32)[None, None, :]
     picked = jnp.sum(jnp.where(chosen, weights_all[:, None, :], 0.0), -1)
-    flat_chosen = chosen.reshape(tok_count * top_count, expert_count).astype(jnp.int32)
-    before = jnp.cumsum(flat_chosen, 0) - flat_chosen
-    order_rank = jnp.sum(before * flat_chosen, -1)
+    pair_count = tok_count * top_count
+    flat_chosen = chosen.reshape(pair_count, expert_count)
+    pair_range = jnp.arange(pair_count, dtype=jnp.int32)
+    earlier = (pair_range[None, :] < pair_range[:, None]).astype(jnp.bfloat16)
+    before = jnp.dot(earlier, flat_chosen.astype(jnp.bfloat16), preferred_element_type=jnp.float32)
+    order_rank = jnp.sum(jnp.where(flat_chosen, before, 0.0), -1).astype(jnp.int32)
     copy_index = order_rank % copy_count
     slot_place = order_rank // copy_count
     table_index = expert_ids.reshape(-1) * copy_count + copy_index

time: 156 us -> 155 us (level)
  no operation moved by 1% of the time
where the time goes in v2:
time: 155 us
  blocking collectives  64.2 us (41%)
  waiting for transfers between devices  51.5 us (33%)
  matrix products  27.4 us (18%)
  starting transfers between devices  5.64 us (4%)
  other arithmetic  2.96 us (2%)
  local copies, waits for them, and re-layouts  2.06 us (1%)
    all_to_all x1, blocking collectives, body(): lax.all_to_all(outgoing, ('dp', 'sub'), split_axis=0, concat_axis=0, tile...  64.2 us
    all_to_all x1, waiting for transfers between devices, body(): lax.all_to_all(answer.reshape(packet.shape), ('dp', 'sub'), split_axis=0,...  51.5 us
    dot_general x1, matrix products, body(): both_rows = jnp.dot(flat_rows, gate_up, preferred_element_type=jnp.float32)  11.4 us
    dot_general x1, matrix products, body(): jnp.dot(hidden, down_proj, preferred_element_type=jnp.float32)  6.15 us
    all_to_all x1, starting transfers between devices, body(): lax.all_to_all(answer.reshape(packet.shape), ('dp', 'sub'), split_axis=0,...  5.64 us
    dot_general x1, matrix products, body(): jnp.dot(attn_heads, out_weight, preferred_element_type=jnp.float32)  5.08 us
  transfers between devices with their start and end apart: 1, of which 1 were waited for; matrix products, arithmetic and copies ran while one was open for 1% of the time, Pallas kernels for 0%

profile of v2, /device:TPU:1, one launch (start us, length us, event | category | flops | bytes accessed | tf_op | source)
XLA Modules:
  0.0 154.6 jit_solution(12550876553837075914)
XLA Ops:
  0.6 0.0 copy-start
  0.6 0.8 copy.19
  1.5 0.1 reshape.102
  1.6 0.3 fusion.13
  1.9 0.8 copy.20
  2.6 0.1 broadcast_in_dim.59
  2.7 0.2 select_reduce_fusion.1
  3.0 0.1 mul.72
  3.1 0.1 convert_element_type.35
  3.2 0.7 fusion.12
  3.9 0.0 copy-start.3
  3.9 5.1 %multiply_reduce_fusion.1 = (f32[64]{0:T(128)S(1)}, f32[64,2048]{1,0:T(8,128)S(1)}) fusion(bf16[64,2048]{1,0:T(8,128)(2,1)S(1)} %copy-done, bf16[2048,2048]{1,0:T(8,128)(2,1)} %param.12, bf16[64,2048]{1,0:T(8,128)(2,1)} %param.11), kind=kOutput, calls=%fused_computation.24 | convolution fusion | flops 537395136 | bytes 9437440 | tf_op jit(solution)/shard_map/dot_general | solution.py:31
  9.0 1.3 convert_bitcast_fusion.1
  10.4 64.2 %all_to_all.10 = bf16[128,8,2048]{2,1,0:T(8,128)(2,1)S(1)} all-to-all(bf16[128,8,2048]{2,1,0:T(8,128)(2,1)S(1)} %convert_bitcast_fusion.1), channel_id=1, replica_groups=mesh['dp'=16,'sub'=8] {'dp','sub'}, dimensions={0} | all-to-all | bytes 8388608 | tf_op jit(solution)/shard_map/all_to_all | solution.py:59
  74.6 11.4 %fusion = f32[1024,2048]{1,0:T(8,128)S(1)} fusion(bf16[1,2048,2048]{2,1,0:T(8,128)(2,1)} %param.17, bf16[128,8,2048]{2,1,0:T(8,128)(2,1)S(1)} %all_to_all.10), kind=kOutput, calls=%fused_computation | convolution fusion | flops 8589934592 | bytes 20971520 | tf_op jit(solution)/shard_map/dot_general | solution.py:61
  86.0 6.2 %convert_bitcast_fusion = bf16[128,8,2048]{2,1,0:T(8,128)(2,1)} fusion(bf16[1,1024,2048]{2,1,0:T(8,128)(2,1)S(1)} %copy-done.6, f32[1024,2048]{1,0:T(8,128)S(1)} %fusion), kind=kOutput, calls=%fused_computation.9 | convolution fusion | flops 4303355904 | bytes 16777216 | tf_op jit(solution)/shard_map/dot_general | solution.py:65
  92.1 5.6 %all-to-all-start.1 = ((bf16[128,8,2048]{2,1,0:T(8,128)(2,1)}), bf16[128,8,2048]{2,1,0:T(8,128)(2,1)}, u32[]{:S(2)}, u32[]{:S(2)}) async-start(bf16[128,8,2048]{2,1,0:T(8,128)(2,1)} %convert_bitcast_fusion), calls=%async_computation.1 | async-start | bytes 8388608 | tf_op jit(solution)/shard_map/all_to_all | solution.py:66
  97.8 0.3 fusion.31
  98.2 0.1 copy.21
  98.3 0.7 select_reduce_fusion
  99.0 51.5 %all-to-all-done.1 = bf16[128,8,2048]{2,1,0:T(8,128)(2,1)} async-done(((bf16[128,8,2048]{2,1,0:T(8,128)(2,1)}), bf16[128,8,2048]{2,1,0:T(8,128)(2,1)}, u32[]{:S(2)}, u32[]{:S(2)}) %all-to-all-start.1) | async-done | bytes 4194336 | tf_op jit(solution)/shard_map/all_to_all | solution.py:66
  150.5 2.9 %fusion.3 = f32[128,2048]{1,0:T(8,128)S(1)} fusion(bf16[128,8,2048]{2,1,0:T(8,128)(2,1)} %all-to-all-done.1, bf16[64,1024]{1,0:T(8,128)(2,1)S(1)} %get-tuple-element.5, bf16[64,1024]{1,0:T(8,128)(2,1)S(1)} %get-tuple-element.4), kind=kOutput, calls=%fused_computation.4 | convolution fusion | flops 537395200 | bytes 5505024 | tf_op jit(solution)/shard_map/dot_general | solution.py:74
  153.4 0.2 multiply_reduce_fusion
  153.7 0.9 multiply_multiply_fusion
  (22 shorter events, 0.2 us)
Async XLA Ops:
  0.6 3.3 %copy-start = (bf16[64,2048]{1,0:T(8,128)(2,1)S(1)}, bf16[64,2048]{1,0:T(8,128)(2,1)}, u32[]{:S(2)}) copy-start(bf16[64,2048]{1,0:T(8,128)(2,1)} %param.10) | copy-start | bytes 786436
  3.9 5.1 %copy-start.3 = (f32[2048]{0:T(1024)S(1)}, f32[2048]{0:T(1024)}, u32[]{:S(2)}) copy-start(f32[2048]{0:T(1024)} %param.13) | copy-start | bytes 24580
  74.6 11.4 %copy-start.6 = (bf16[1,1024,2048]{2,1,0:T(8,128)(2,1)S(1)}, bf16[1,1024,2048]{2,1,0:T(8,128)(2,1)}, u32[]{:S(2)}) copy-start(bf16[1,1024,2048]{2,1,0:T(8,128)(2,1)} %param.18) | copy-start | bytes 12582916
  92.1 5.7 %copy-start.2 = (bf16[2048,32]{0,1:T(8,128)(2,1)S(1)}, bf16[2048,32]{0,1:T(8,128)(2,1)}, u32[]{:S(2)}) copy-start(bf16[2048,32]{0,1:T(8,128)(2,1)} %param.14) | copy-start | bytes 393220
  92.1 6.0 %copy-start.4 = (s32[64,8]{0,1:T(8,128)S(1)}, s32[64,8]{0,1:T(8,128)}, u32[]{:S(2)}) copy-start(s32[64,8]{0,1:T(8,128)} %param.15) | copy-start | bytes 6148
  92.1 58.4 %all-to-all-start.1 = ((bf16[128,8,2048]{2,1,0:T(8,128)(2,1)}), bf16[128,8,2048]{2,1,0:T(8,128)(2,1)}, u32[]{:S(2)}, u32[]{:S(2)}) async-start(bf16[128,8,2048]{2,1,0:T(8,128)(2,1)} %convert_bitcast_fusion), calls=%async_computation.1 | async-start | bytes 8388608 | tf_op jit(solution)/shard_map/all_to_all | solution.py:66
  98.3 55.4 %copy-start.5 = (f32[2048]{0:T(1024)S(1)}, f32[2048]{0:T(1024)}, u32[]{:S(2)}) copy-start(f32[2048]{0:T(1024)} %param.19) | copy-start | bytes 24580
  153.6 1.0 copy-start.1

commit v3 on v2

--- a/solution.py
+++ b/solution.py
@@ -1,11 +1,59 @@
+import functools
+
 import jax
 import jax.numpy as jnp
 from jax import lax
+from jax.experimental import pallas as pl
+from jax.experimental.pallas import tpu as pltpu
 from jax.sharding import PartitionSpec as P
 
 
 def rms_factor(widened):
     return lax.rsqrt(jnp.mean(widened * widened, -1, keepdims=True) + 1e-05)
+
+
+def project_kernel(block, attn_ref, resid_ref, weight_ref, gain_ref, stream_ref, normed_ref, held):
+    step = pl.program_id(0)
+    part = jnp.dot(attn_ref[...], weight_ref[...], preferred_element_type=jnp.float32)
+    part = resid_ref[...].astype(jnp.float32) + part
+    stream_ref[...] = part
+    held[:, pl.ds(pl.multiple_of(step * block, block), block)] = part
+
+    @pl.when(step == pl.num_programs(0) - 1)
+    def _():
+        whole = held[...]
+        factor = lax.rsqrt(jnp.mean(whole * whole, -1, keepdims=True) + 1e-05)
+        normed_ref[...] = (whole * factor * gain_ref[...]).astype(normed_ref.dtype)
+
+
+def project(attn_heads, residual, out_weight, norm_gain):
+    rows, width = attn_heads.shape
+    block = 512
+    return pl.pallas_call(
+        functools.partial(project_kernel, block),
+        grid=(width // block,),
+        in_specs=[
+            pl.BlockSpec((rows, width), lambda j: (0, 0)),
+            pl.BlockSpec((rows, block), lambda j: (0, j)),
+            pl.BlockSpec((width, block), lambda j: (0, j)),
+            pl.BlockSpec((1, width), lambda j: (0, 0)),
+        ],
+        out_specs=[
+            pl.BlockSpec((rows, block), lambda j: (0, j)),
+            pl.BlockSpec((rows, width), lambda j: (0, 0)),
+        ],
+        out_shape=[
+            jax.ShapeDtypeStruct((rows, width), jnp.float32),
+            jax.ShapeDtypeStruct((rows, width), jnp.bfloat16),
+        ],
+        scratch_shapes=[pltpu.VMEM((rows, width), jnp.float32)],
+        compiler_params=pltpu.CompilerParams(dimension_semantics=("arbitrary",)),
+        cost_estimate=pl.CostEstimate(
+            flops=2 * rows * width * width,
+            transcendentals=rows,
+            bytes_accessed=2 * width * width + 2 * 2 * rows * width + 6 * rows * width,
+        ),
+    )(attn_heads, residual, out_weight, norm_gain.reshape(1, width))
 
 
 def body(
@@ -28,9 +76,7 @@
     capacity = 2 * tok_count * top_count // expert_count
     per_slot = capacity // copy_count
     slot_count = device_count * per_slot
-    projected = jnp.dot(attn_heads, out_weight, preferred_element_type=jnp.float32)
-    stream = residual.astype(jnp.float32) + projected
-    normed = (stream * rms_factor(stream) * norm_gain).astype(jnp.bfloat16)
+    stream, normed = project(attn_heads, residual, out_weight, norm_gain)
     logits = jnp.dot(normed, router_weight, preferred_element_type=jnp.float32)
     weights_all = jax.nn.softmax(logits, axis=-1)
     chosen = expert_ids[:, :, None] == jnp.arange(expert_count, dtype=jnp.int32)[None, None, :]

time: 155 us -> 157 us (1.013)
  Pallas kernels: 0 us -> 6.11 us
  matrix products: 27.4 us -> 23.2 us
    pallas_call x0 -> x1, Pallas kernels: none -> 6.11 us  [project(): pl.pallas_call(functools.partial(project_kernel, block), grid=(width // b...]
    dot_general x1 -> x0, matrix products: 5.08 us -> none  [body(): jnp.dot(attn_heads, out_weight, preferred_element_type=jnp.float32)]
where the time goes in v3:
time: 157 us
  blocking collectives  64.2 us (41%)
  waiting for transfers between devices  51.5 us (33%)
  matrix products  23.2 us (15%)
  Pallas kernels  6.11 us (4%)
  starting transfers between devices  5.64 us (4%)
  other arithmetic  2.95 us (2%)
  local copies, waits for them, and re-layouts  2.05 us (1%)
    all_to_all x1, blocking collectives, body(): lax.all_to_all(outgoing, ('dp', 'sub'), split_axis=0, concat_axis=0, tile...  64.2 us
    all_to_all x1, waiting for transfers between devices, body(): lax.all_to_all(answer.reshape(packet.shape), ('dp', 'sub'), split_axis=0,...  51.5 us
    dot_general x1, matrix products, body(): both_rows = jnp.dot(flat_rows, gate_up, preferred_element_type=jnp.float32)  11.4 us
    dot_general x1, matrix products, body(): jnp.dot(hidden, down_proj, preferred_element_type=jnp.float32)  6.15 us
    pallas_call x1, Pallas kernels, project(): pl.pallas_call(functools.partial(project_kernel, block), grid=(width // b...  6.11 us
    all_to_all x1, starting transfers between devices, body(): lax.all_to_all(answer.reshape(packet.shape), ('dp', 'sub'), split_axis=0,...  5.64 us
  transfers between devices with their start and end apart: 1, of which 1 were waited for; matrix products, arithmetic and copies ran while one was open for 1% of the time, Pallas kernels for 0%

profile of v3, /device:TPU:1, one launch (start us, length us, event | category | flops | bytes accessed | tf_op | source)
XLA Modules:
  0.0 156.5 jit_solution(2351275227560550950)
XLA Ops:
  0.6 0.0 copy-start
  0.6 0.8 copy.19
  1.5 0.1 reshape.97
  1.5 0.3 fusion.13
  1.9 0.8 copy.20
  2.6 0.1 broadcast_in_dim.57
  2.7 0.2 select_reduce_fusion.1
  3.0 0.1 convert_element_type.28
  3.1 0.1 mul.53
  3.2 0.7 fusion.12
  3.9 6.1 %shard_map.113 = (f32[64,2048]{1,0:T(8,128)}, bf16[64,2048]{1,0:T(8,128)(2,1)}) custom-call(bf16[64,2048]{1,0:T(8,128)(2,1)} %attn_ref.1, bf16[64,2048]{1,0:T(8,128)(2,1)} %resid_ref.1, bf16[2048,2048]{1,0:T(8,128)(2,1)} %weight_ref.1, f32[1,2048]{1,0:T(1,128)} %bitcast.26), custom_call_target="tpu_custom_call" | custom-call | flops 536870912 | bytes 9699328 | tf_op jit(solution)/shard_map/pallas_call | solution.py:32
  10.0 2.2 %convert_bitcast_fusion.1 = bf16[128,8,2048]{2,1,0:T(8,128)(2,1)S(1)} fusion(pred[1024,64]{0,1:T(8,128)(4,1)S(1)} %fusion.12, bf16[64,2048]{1,0:T(8,128)(2,1)} %get-tuple-element.5), kind=kOutput, calls=%fused_computation.10 | convolution fusion | flops 270532608 | bytes 4521984 | tf_op jit(solution)/shard_map/dot_general | solution.py:101
  12.2 64.2 %all_to_all.10 = bf16[128,8,2048]{2,1,0:T(8,128)(2,1)S(1)} all-to-all(bf16[128,8,2048]{2,1,0:T(8,128)(2,1)S(1)} %convert_bitcast_fusion.1), channel_id=1, replica_groups=mesh['dp'=16,'sub'=8] {'dp','sub'}, dimensions={0} | all-to-all | bytes 8388608 | tf_op jit(solution)/shard_map/all_to_all | solution.py:105
  76.5 11.4 %fusion = f32[1024,2048]{1,0:T(8,128)S(1)} fusion(bf16[1,2048,2048]{2,1,0:T(8,128)(2,1)} %param.17, bf16[128,8,2048]{2,1,0:T(8,128)(2,1)S(1)} %all_to_all.10), kind=kOutput, calls=%fused_computation | convolution fusion | flops 8589934592 | bytes 20971520 | tf_op jit(solution)/shard_map/dot_general | solution.py:107
  87.9 6.2 %convert_bitcast_fusion = bf16[128,8,2048]{2,1,0:T(8,128)(2,1)} fusion(bf16[1,1024,2048]{2,1,0:T(8,128)(2,1)S(1)} %copy-done.6, f32[1024,2048]{1,0:T(8,128)S(1)} %fusion), kind=kOutput, calls=%fused_computation.9 | convolution fusion | flops 4303355904 | bytes 16777216 | tf_op jit(solution)/shard_map/dot_general | solution.py:111
  94.0 5.6 %all-to-all-start.1 = ((bf16[128,8,2048]{2,1,0:T(8,128)(2,1)}), bf16[128,8,2048]{2,1,0:T(8,128)(2,1)}, u32[]{:S(2)}, u32[]{:S(2)}) async-start(bf16[128,8,2048]{2,1,0:T(8,128)(2,1)} %convert_bitcast_fusion), calls=%async_computation.1 | async-start | bytes 8388608 | tf_op jit(solution)/shard_map/all_to_all | solution.py:112
  99.7 0.0 copy-start.3
  99.7 0.2 fusion.30
  100.0 0.1 copy.21
  100.1 0.7 select_reduce_fusion
  100.9 51.5 %all-to-all-done.1 = bf16[128,8,2048]{2,1,0:T(8,128)(2,1)} async-done(((bf16[128,8,2048]{2,1,0:T(8,128)(2,1)}), bf16[128,8,2048]{2,1,0:T(8,128)(2,1)}, u32[]{:S(2)}, u32[]{:S(2)}) %all-to-all-start.1) | async-done | bytes 4194336 | tf_op jit(solution)/shard_map/all_to_all | solution.py:112
  152.4 2.9 %fusion.3 = f32[128,2048]{1,0:T(8,128)S(1)} fusion(bf16[128,8,2048]{2,1,0:T(8,128)(2,1)} %all-to-all-done.1, bf16[64,1024]{1,0:T(8,128)(2,1)S(1)} %get-tuple-element.9, bf16[64,1024]{1,0:T(8,128)(2,1)S(1)} %get-tuple-element.8), kind=kOutput, calls=%fused_computation.4 | convolution fusion | flops 537395200 | bytes 5505024 | tf_op jit(solution)/shard_map/dot_general | solution.py:120
  155.3 0.2 multiply_reduce_fusion
  155.6 0.9 multiply_multiply_fusion
  (21 shorter events, 0.2 us)
Async XLA Ops:
  0.6 99.1 %copy-start = (bf16[2048,32]{0,1:T(8,128)(2,1)S(1)}, bf16[2048,32]{0,1:T(8,128)(2,1)}, u32[]{:S(2)}) copy-start(bf16[2048,32]{0,1:T(8,128)(2,1)} %param.14) | copy-start | bytes 393220
  76.5 11.4 %copy-start.6 = (bf16[1,1024,2048]{2,1,0:T(8,128)(2,1)S(1)}, bf16[1,1024,2048]{2,1,0:T(8,128)(2,1)}, u32[]{:S(2)}) copy-start(bf16[1,1024,2048]{2,1,0:T(8,128)(2,1)} %param.18) | copy-start | bytes 12582916
  94.0 5.7 %copy-start.2 = (bf16[64,2048]{1,0:T(8,128)(2,1)S(1)}, bf16[64,2048]{1,0:T(8,128)(2,1)}, u32[]{:S(2)}) copy-start(bf16[64,2048]{1,0:T(8,128)(2,1)} %get-tuple-element.5) | copy-start | bytes 786436
  94.0 6.0 %copy-start.4 = (s32[64,8]{0,1:T(8,128)S(1)}, s32[64,8]{0,1:T(8,128)}, u32[]{:S(2)}) copy-start(s32[64,8]{0,1:T(8,128)} %param.15) | copy-start | bytes 6148
  94.0 58.4 %all-to-all-start.1 = ((bf16[128,8,2048]{2,1,0:T(8,128)(2,1)}), bf16[128,8,2048]{2,1,0:T(8,128)(2,1)}, u32[]{:S(2)}, u32[]{:S(2)}) async-start(bf16[128,8,2048]{2,1,0:T(8,128)(2,1)} %convert_bitcast_fusion), calls=%async_computation.1 | async-start | bytes 8388608 | tf_op jit(solution)/shard_map/all_to_all | solution.py:112
  99.7 55.6 %copy-start.3 = (f32[64,2048]{1,0:T(8,128)S(1)}, f32[64,2048]{1,0:T(8,128)}, u32[]{:S(2)}) copy-start(f32[64,2048]{1,0:T(8,128)} %get-tuple-element.4) | copy-start | bytes 1572868
  100.1 55.4 %copy-start.5 = (f32[2048]{0:T(1024)S(1)}, f32[2048]{0:T(1024)}, u32[]{:S(2)}) copy-start(f32[2048]{0:T(1024)} %param.19) | copy-start | bytes 24580
  155.5 1.0 copy-start.1

commit v4 on v3

--- a/solution.py
+++ b/solution.py
@@ -1,5 +1,3 @@
-import functools
-
 import jax
 import jax.numpy as jnp
 from jax import lax
@@ -12,16 +10,22 @@
     return lax.rsqrt(jnp.mean(widened * widened, -1, keepdims=True) + 1e-05)
 
 
-def project_kernel(block, attn_ref, resid_ref, weight_ref, gain_ref, stream_ref, normed_ref, held):
+def project_kernel(attn_ref, weight_ref, resid_ref, gain_ref, stream_ref, normed_ref, total):
     step = pl.program_id(0)
     part = jnp.dot(attn_ref[...], weight_ref[...], preferred_element_type=jnp.float32)
-    part = resid_ref[...].astype(jnp.float32) + part
-    stream_ref[...] = part
-    held[:, pl.ds(pl.multiple_of(step * block, block), block)] = part
+
+    @pl.when(step == 0)
+    def _():
+        total[...] = part
+
+    @pl.when(step > 0)
+    def _():
+        total[...] += part
 
     @pl.when(step == pl.num_programs(0) - 1)
     def _():
-        whole = held[...]
+        whole = resid_ref[...].astype(jnp.float32) + total[...]
+        stream_ref[...] = whole
         factor = lax.rsqrt(jnp.mean(whole * whole, -1, keepdims=True) + 1e-05)
         normed_ref[...] = (whole * factor * gain_ref[...]).astype(normed_ref.dtype)
 
@@ -30,17 +34,17 @@
     rows, width = attn_heads.shape
     block = 512
     return pl.pallas_call(
-        functools.partial(project_kernel, block),
+        project_kernel,
         grid=(width // block,),
         in_specs=[
-            pl.BlockSpec((rows, width), lambda j: (0, 0)),
-            pl.BlockSpec((rows, block), lambda j: (0, j)),
-            pl.BlockSpec((width, block), lambda j: (0, j)),
-            pl.BlockSpec((1, width), lambda j: (0, 0)),
+            pl.BlockSpec((rows, block), lambda k: (0, k)),
+            pl.BlockSpec((block, width), lambda k: (k, 0)),
+            pl.BlockSpec((rows, width), lambda k: (0, 0)),
+            pl.BlockSpec((1, width), lambda k: (0, 0)),
         ],
         out_specs=[
-            pl.BlockSpec((rows, block), lambda j: (0, j)),
-            pl.BlockSpec((rows, width), lambda j: (0, 0)),
+            pl.BlockSpec((rows, width), lambda k: (0, 0)),
+            pl.BlockSpec((rows, width), lambda k: (0, 0)),
         ],
         out_shape=[
             jax.ShapeDtypeStruct((rows, width), jnp.float32),
@@ -53,7 +57,7 @@
             transcendentals=rows,
             bytes_accessed=2 * width * width + 2 * 2 * rows * width + 6 * rows * width,
         ),
-    )(attn_heads, residual, out_weight, norm_gain.reshape(1, width))
+    )(attn_heads, out_weight, residual, norm_gain.reshape(1, width))
 
 
 def body(

time: 157 us -> 157 us (level)
  no operation moved by 1% of the time
where the time goes in v4:
time: 157 us
  blocking collectives  64.2 us (41%)
  waiting for transfers between devices  51.5 us (33%)
  matrix products  23.2 us (15%)
  Pallas kernels  6.29 us (4%)
  starting transfers between devices  5.64 us (4%)
  other arithmetic  2.95 us (2%)
  local copies, waits for them, and re-layouts  2.05 us (1%)
    all_to_all x1, blocking collectives, body(): lax.all_to_all(outgoing, ('dp', 'sub'), split_axis=0, concat_axis=0, tile...  64.2 us
    all_to_all x1, waiting for transfers between devices, body(): lax.all_to_all(answer.reshape(packet.shape), ('dp', 'sub'), split_axis=0,...  51.5 us
    dot_general x1, matrix products, body(): both_rows = jnp.dot(flat_rows, gate_up, preferred_element_type=jnp.float32)  11.4 us
    pallas_call x1, Pallas kernels, project(): pl.pallas_call(project_kernel, grid=(width // block,), in_specs=[pl.Block...  6.29 us
    dot_general x1, matrix products, body(): jnp.dot(hidden, down_proj, preferred_element_type=jnp.float32)  6.15 us
    all_to_all x1, starting transfers between devices, body(): lax.all_to_all(answer.reshape(packet.shape), ('dp', 'sub'), split_axis=0,...  5.64 us
  transfers between devices with their start and end apart: 1, of which 1 were waited for; matrix products, arithmetic and copies ran while one was open for 1% of the time, Pallas kernels for 0%

profile of v4, /device:TPU:1, one launch (start us, length us, event | category | flops | bytes accessed | tf_op | source)
XLA Modules:
  0.0 156.7 jit_solution(5437629409853158667)
XLA Ops:
  0.6 0.0 copy-start
  0.6 0.8 copy.19
  1.5 0.1 reshape.97
  1.5 0.3 fusion.13
  1.9 0.8 copy.20
  2.6 0.1 broadcast_in_dim.57
  2.7 0.2 select_reduce_fusion.1
  3.0 0.1 convert_element_type.28
  3.1 0.1 mul.53
  3.2 0.7 fusion.12
  3.9 6.3 %shard_map.113 = (f32[64,2048]{1,0:T(8,128)}, bf16[64,2048]{1,0:T(8,128)(2,1)}) custom-call(bf16[64,2048]{1,0:T(8,128)(2,1)} %attn_ref.1, bf16[2048,2048]{1,0:T(8,128)(2,1)} %weight_ref.1, bf16[64,2048]{1,0:T(8,128)(2,1)} %resid_ref.1, f32[1,2048]{1,0:T(1,128)} %bitcast.26), custom_call_target="tpu_custom_call" | custom-call | flops 536870912 | bytes 9699328 | tf_op jit(solution)/shard_map/pallas_call | solution.py:36
  10.2 2.2 %convert_bitcast_fusion.1 = bf16[128,8,2048]{2,1,0:T(8,128)(2,1)S(1)} fusion(pred[1024,64]{0,1:T(8,128)(4,1)S(1)} %fusion.12, bf16[64,2048]{1,0:T(8,128)(2,1)} %get-tuple-element.5), kind=kOutput, calls=%fused_computation.10 | convolution fusion | flops 270532608 | bytes 4521984 | tf_op jit(solution)/shard_map/dot_general | solution.py:105
  12.4 64.2 %all_to_all.10 = bf16[128,8,2048]{2,1,0:T(8,128)(2,1)S(1)} all-to-all(bf16[128,8,2048]{2,1,0:T(8,128)(2,1)S(1)} %convert_bitcast_fusion.1), channel_id=1, replica_groups=mesh['dp'=16,'sub'=8] {'dp','sub'}, dimensions={0} | all-to-all | bytes 8388608 | tf_op jit(solution)/shard_map/all_to_all | solution.py:109
  76.7 11.4 %fusion = f32[1024,2048]{1,0:T(8,128)S(1)} fusion(bf16[1,2048,2048]{2,1,0:T(8,128)(2,1)} %param.17, bf16[128,8,2048]{2,1,0:T(8,128)(2,1)S(1)} %all_to_all.10), kind=kOutput, calls=%fused_computation | convolution fusion | flops 8589934592 | bytes 20971520 | tf_op jit(solution)/shard_map/dot_general | solution.py:111
  88.1 6.2 %convert_bitcast_fusion = bf16[128,8,2048]{2,1,0:T(8,128)(2,1)} fusion(bf16[1,1024,2048]{2,1,0:T(8,128)(2,1)S(1)} %copy-done.6, f32[1024,2048]{1,0:T(8,128)S(1)} %fusion), kind=kOutput, calls=%fused_computation.9 | convolution fusion | flops 4303355904 | bytes 16777216 | tf_op jit(solution)/shard_map/dot_general | solution.py:115
  94.2 5.6 %all-to-all-start.1 = ((bf16[128,8,2048]{2,1,0:T(8,128)(2,1)}), bf16[128,8,2048]{2,1,0:T(8,128)(2,1)}, u32[]{:S(2)}, u32[]{:S(2)}) async-start(bf16[128,8,2048]{2,1,0:T(8,128)(2,1)} %convert_bitcast_fusion), calls=%async_computation.1 | async-start | bytes 8388608 | tf_op jit(solution)/shard_map/all_to_all | solution.py:116
  99.9 0.0 copy-start.3
  99.9 0.2 fusion.30
  100.2 0.1 copy.21
  100.3 0.7 select_reduce_fusion
  101.1 51.5 %all-to-all-done.1 = bf16[128,8,2048]{2,1,0:T(8,128)(2,1)} async-done(((bf16[128,8,2048]{2,1,0:T(8,128)(2,1)}), bf16[128,8,2048]{2,1,0:T(8,128)(2,1)}, u32[]{:S(2)}, u32[]{:S(2)}) %all-to-all-start.1) | async-done | bytes 4194336 | tf_op jit(solution)/shard_map/all_to_all | solution.py:116
  152.6 2.9 %fusion.3 = f32[128,2048]{1,0:T(8,128)S(1)} fusion(bf16[128,8,2048]{2,1,0:T(8,128)(2,1)} %all-to-all-done.1, bf16[64,1024]{1,0:T(8,128)(2,1)S(1)} %get-tuple-element.9, bf16[64,1024]{1,0:T(8,128)(2,1)S(1)} %get-tuple-element.8), kind=kOutput, calls=%fused_computation.4 | convolution fusion | flops 537395200 | bytes 5505024 | tf_op jit(solution)/shard_map/dot_general | solution.py:124
  155.5 0.2 multiply_reduce_fusion
  155.7 0.9 multiply_multiply_fusion
  (21 shorter events, 0.2 us)
Async XLA Ops:
  0.6 99.2 %copy-start = (bf16[2048,32]{0,1:T(8,128)(2,1)S(1)}, bf16[2048,32]{0,1:T(8,128)(2,1)}, u32[]{:S(2)}) copy-start(bf16[2048,32]{0,1:T(8,128)(2,1)} %param.14) | copy-start | bytes 393220
  76.7 11.4 %copy-start.6 = (bf16[1,1024,2048]{2,1,0:T(8,128)(2,1)S(1)}, bf16[1,1024,2048]{2,1,0:T(8,128)(2,1)}, u32[]{:S(2)}) copy-start(bf16[1,1024,2048]{2,1,0:T(8,128)(2,1)} %param.18) | copy-start | bytes 12582916
  94.2 5.7 %copy-start.2 = (bf16[64,2048]{1,0:T(8,128)(2,1)S(1)}, bf16[64,2048]{1,0:T(8,128)(2,1)}, u32[]{:S(2)}) copy-start(bf16[64,2048]{1,0:T(8,128)(2,1)} %get-tuple-element.5) | copy-start | bytes 786436
  94.2 6.0 %copy-start.4 = (s32[64,8]{0,1:T(8,128)S(1)}, s32[64,8]{0,1:T(8,128)}, u32[]{:S(2)}) copy-start(s32[64,8]{0,1:T(8,128)} %param.15) | copy-start | bytes 6148
  94.2 58.4 %all-to-all-start.1 = ((bf16[128,8,2048]{2,1,0:T(8,128)(2,1)}), bf16[128,8,2048]{2,1,0:T(8,128)(2,1)}, u32[]{:S(2)}, u32[]{:S(2)}) async-start(bf16[128,8,2048]{2,1,0:T(8,128)(2,1)} %convert_bitcast_fusion), calls=%async_computation.1 | async-start | bytes 8388608 | tf_op jit(solution)/shard_map/all_to_all | solution.py:116
  99.9 55.6 %copy-start.3 = (f32[64,2048]{1,0:T(8,128)S(1)}, f32[64,2048]{1,0:T(8,128)}, u32[]{:S(2)}) copy-start(f32[64,2048]{1,0:T(8,128)} %get-tuple-element.4) | copy-start | bytes 1572868
  100.3 55.4 %copy-start.5 = (f32[2048]{0:T(1024)S(1)}, f32[2048]{0:T(1024)}, u32[]{:S(2)}) copy-start(f32[2048]{0:T(1024)} %param.19) | copy-start | bytes 24580
  155.7 1.0 copy-start.1

commit v5 on v2

--- a/solution.py
+++ b/solution.py
@@ -30,6 +30,7 @@
     slot_count = device_count * per_slot
     projected = jnp.dot(attn_heads, out_weight, preferred_element_type=jnp.float32)
     stream = residual.astype(jnp.float32) + projected
+    stream = lax.optimization_barrier(stream)
     normed = (stream * rms_factor(stream) * norm_gain).astype(jnp.bfloat16)
     logits = jnp.dot(normed, router_weight, preferred_element_type=jnp.float32)
     weights_all = jax.nn.softmax(logits, axis=-1)

time: 155 us -> 152 us (0.981)
  matrix products: 27.4 us -> 24.8 us
    dot_general x1, matrix products: 11.4 us -> 8.89 us  [body(): both_rows = jnp.dot(flat_rows, gate_up, preferred_element_type=jnp.float32)]
where the time goes in v5:
time: 152 us; the launch traced here: 151 us
  blocking collectives  64.2 us (42%)
  waiting for transfers between devices  51.5 us (34%)
  matrix products  24.8 us (16%)
  starting transfers between devices  5.64 us (4%)
  other arithmetic  3.1 us (2%)
    all_to_all x1, blocking collectives, body(): lax.all_to_all(outgoing, ('dp', 'sub'), split_axis=0, concat_axis=0, tile...  64.2 us
    all_to_all x1, waiting for transfers between devices, body(): lax.all_to_all(answer.reshape(packet.shape), ('dp', 'sub'), split_axis=0,...  51.5 us
    dot_general x1, matrix products, body(): both_rows = jnp.dot(flat_rows, gate_up, preferred_element_type=jnp.float32)  8.89 us
    dot_general x1, matrix products, body(): jnp.dot(hidden, down_proj, preferred_element_type=jnp.float32)  6.14 us
    all_to_all x1, starting transfers between devices, body(): lax.all_to_all(answer.reshape(packet.shape), ('dp', 'sub'), split_axis=0,...  5.64 us
    dot_general x1, matrix products, body(): jnp.dot(attn_heads, out_weight, preferred_element_type=jnp.float32)  4.96 us
  transfers between devices with their start and end apart: 1, of which 1 were waited for; matrix products, arithmetic and copies ran while one was open for 1% of the time, Pallas kernels for 0%

profile of v5, /device:TPU:1, one launch (start us, length us, event | category | flops | bytes accessed | tf_op | source)
XLA Modules:
  0.0 151.5 jit_solution(5700265303454845204)
XLA Ops:
  0.6 0.0 copy-start
  0.6 0.8 copy.19
  1.5 0.1 reshape.102
  1.6 0.3 fusion.13
  1.9 5.0 %convolution_add_fusion = f32[64,2048]{1,0:T(8,128)S(1)} fusion(bf16[64,2048]{1,0:T(8,128)(2,1)S(1)} %copy-done, bf16[2048,2048]{1,0:T(8,128)(2,1)} %param.12, bf16[64,2048]{1,0:T(8,128)(2,1)} %param.11), kind=kOutput, calls=%fused_computation.11 | convolution fusion | flops 537133056 | bytes 9437184 | tf_op jit(solution)/shard_map/dot_general | solution.py:31
  6.9 0.1 copy.20
  7.0 0.1 broadcast_in_dim.59
  7.1 0.2 select_reduce_fusion.1
  7.3 0.1 mul.72
  7.4 0.1 convert_element_type.35
  7.5 0.7 fusion.12
  8.2 0.1 multiply_reduce_fusion.1
  8.4 1.3 convert_bitcast_fusion.1
  9.7 64.2 %all_to_all.10 = bf16[128,8,2048]{2,1,0:T(8,128)(2,1)S(1)} all-to-all(bf16[128,8,2048]{2,1,0:T(8,128)(2,1)S(1)} %convert_bitcast_fusion.1), channel_id=1, replica_groups=mesh['dp'=16,'sub'=8] {'dp','sub'}, dimensions={0} | all-to-all | bytes 8388608 | tf_op jit(solution)/shard_map/all_to_all | solution.py:60
  74.0 8.9 %fusion = f32[1024,2048]{1,0:T(8,128)S(1)} fusion(bf16[1,2048,2048]{2,1,0:T(8,128)(2,1)S(1)} %copy-done.7, bf16[128,8,2048]{2,1,0:T(8,128)(2,1)S(1)} %all_to_all.10), kind=kOutput, calls=%fused_computation | convolution fusion | flops 8589934592 | bytes 20971520 | tf_op jit(solution)/shard_map/dot_general | solution.py:62
  82.9 6.1 %convert_bitcast_fusion = bf16[128,8,2048]{2,1,0:T(8,128)(2,1)} fusion(bf16[1,1024,2048]{2,1,0:T(8,128)(2,1)S(1)} %copy-done.8, f32[1024,2048]{1,0:T(8,128)S(1)} %fusion), kind=kOutput, calls=%fused_computation.9 | convolution fusion | flops 4303355904 | bytes 16777216 | tf_op jit(solution)/shard_map/dot_general | solution.py:66
  89.0 5.6 %all-to-all-start.1 = ((bf16[128,8,2048]{2,1,0:T(8,128)(2,1)}), bf16[128,8,2048]{2,1,0:T(8,128)(2,1)}, u32[]{:S(2)}, u32[]{:S(2)}) async-start(bf16[128,8,2048]{2,1,0:T(8,128)(2,1)} %convert_bitcast_fusion), calls=%async_computation.1 | async-start | bytes 8388608 | tf_op jit(solution)/shard_map/all_to_all | solution.py:67
  94.7 0.3 fusion.31
  95.1 0.1 copy.21
  95.1 0.7 select_reduce_fusion
  95.9 51.5 %all-to-all-done.1 = bf16[128,8,2048]{2,1,0:T(8,128)(2,1)} async-done(((bf16[128,8,2048]{2,1,0:T(8,128)(2,1)}), bf16[128,8,2048]{2,1,0:T(8,128)(2,1)}, u32[]{:S(2)}, u32[]{:S(2)}) %all-to-all-start.1) | async-done | bytes 4194336 | tf_op jit(solution)/shard_map/all_to_all | solution.py:67
  147.4 2.9 %fusion.3 = f32[128,2048]{1,0:T(8,128)S(1)} fusion(bf16[128,8,2048]{2,1,0:T(8,128)(2,1)} %all-to-all-done.1, bf16[64,1024]{1,0:T(8,128)(2,1)S(1)} %get-tuple-element.5, bf16[64,1024]{1,0:T(8,128)(2,1)S(1)} %get-tuple-element.4), kind=kOutput, calls=%fused_computation.4 | convolution fusion | flops 537395200 | bytes 5505024 | tf_op jit(solution)/shard_map/dot_general | solution.py:75
  150.3 0.2 multiply_reduce_fusion
  150.5 0.9 multiply_multiply_fusion
  (27 shorter events, 0.2 us)
Async XLA Ops:
  0.6 1.2 copy-start
  1.9 5.0 %copy-start.6 = (s32[32,4]{0,1:T(4,128)S(1)}, s32[32,4]{0,1:T(4,128)}, u32[]{:S(2)}) copy-start(s32[32,4]{0,1:T(4,128)} %param.16) | copy-start | bytes 1540
  1.9 6.5 %copy-start.3 = (f32[2048]{0:T(1024)S(1)}, f32[2048]{0:T(1024)}, u32[]{:S(2)}) copy-start(f32[2048]{0:T(1024)} %param.13) | copy-start | bytes 24580
  9.7 64.2 %copy-start.7 = (bf16[1,2048,2048]{2,1,0:T(8,128)(2,1)S(1)}, bf16[1,2048,2048]{2,1,0:T(8,128)(2,1)}, u32[]{:S(2)}) copy-start(bf16[1,2048,2048]{2,1,0:T(8,128)(2,1)} %param.17) | copy-start | bytes 25165828
  74.0 8.9 %copy-start.8 = (bf16[1,1024,2048]{2,1,0:T(8,128)(2,1)S(1)}, bf16[1,1024,2048]{2,1,0:T(8,128)(2,1)}, u32[]{:S(2)}) copy-start(bf16[1,1024,2048]{2,1,0:T(8,128)(2,1)} %param.18) | copy-start | bytes 12582916
  89.0 5.6 %copy-start.2 = (bf16[2048,32]{0,1:T(8,128)(2,1)S(1)}, bf16[2048,32]{0,1:T(8,128)(2,1)}, u32[]{:S(2)}) copy-start(bf16[2048,32]{0,1:T(8,128)(2,1)} %param.14) | copy-start | bytes 393220
  89.0 6.0 %copy-start.4 = (s32[64,8]{0,1:T(8,128)S(1)}, s32[64,8]{0,1:T(8,128)}, u32[]{:S(2)}) copy-start(s32[64,8]{0,1:T(8,128)} %param.15) | copy-start | bytes 6148
  89.0 58.4 %all-to-all-start.1 = ((bf16[128,8,2048]{2,1,0:T(8,128)(2,1)}), bf16[128,8,2048]{2,1,0:T(8,128)(2,1)}, u32[]{:S(2)}, u32[]{:S(2)}) async-start(bf16[128,8,2048]{2,1,0:T(8,128)(2,1)} %convert_bitcast_fusion), calls=%async_computation.1 | async-start | bytes 8388608 | tf_op jit(solution)/shard_map/all_to_all | solution.py:67
  95.1 55.4 %copy-start.5 = (f32[2048]{0:T(1024)S(1)}, f32[2048]{0:T(1024)}, u32[]{:S(2)}) copy-start(f32[2048]{0:T(1024)} %param.19) | copy-start | bytes 24580
  150.5 1.0 copy-start.1

commit v6 on v5

--- a/solution.py
+++ b/solution.py
@@ -63,6 +63,7 @@
     hidden = (jax.nn.silu(both_rows[:, :hidden_width]) * both_rows[:, hidden_width:]).astype(
         jnp.bfloat16
     )
+    hidden = lax.optimization_barrier(hidden)
     answer = jnp.dot(hidden, down_proj, preferred_element_type=jnp.float32).astype(jnp.bfloat16)
     returned = lax.all_to_all(
         answer.reshape(packet.shape), ("dp", "sub"), split_axis=0, concat_axis=0, tiled=True

time: 152 us -> 154 us (1.013)
  no operation moved by 1% of the time
where the time goes in v6:
time: 154 us
  blocking collectives  64.2 us (42%)
  waiting for transfers between devices  51.5 us (33%)
  matrix products  24.7 us (16%)
  starting transfers between devices  5.64 us (4%)
  other arithmetic  4.53 us (3%)
  local copies, waits for them, and re-layouts  2.14 us (1%)
    all_to_all x1, blocking collectives, body(): lax.all_to_all(outgoing, ('dp', 'sub'), split_axis=0, concat_axis=0, tile...  64.2 us
    all_to_all x1, waiting for transfers between devices, body(): lax.all_to_all(answer.reshape(packet.shape), ('dp', 'sub'), split_axis=0,...  51.5 us
    dot_general x1, matrix products, body(): both_rows = jnp.dot(flat_rows, gate_up, preferred_element_type=jnp.float32)  8.89 us
    dot_general x1, matrix products, body(): jnp.dot(hidden, down_proj, preferred_element_type=jnp.float32)  6.08 us
    all_to_all x1, starting transfers between devices, body(): lax.all_to_all(answer.reshape(packet.shape), ('dp', 'sub'), split_axis=0,...  5.64 us
    dot_general x1, matrix products, body(): jnp.dot(attn_heads, out_weight, preferred_element_type=jnp.float32)  4.96 us
  transfers between devices with their start and end apart: 1, of which 1 were waited for; matrix products, arithmetic and copies ran while one was open for 1% of the time, Pallas kernels for 0%

profile of v6, /device:TPU:1, one launch (start us, length us, event | category | flops | bytes accessed | tf_op | source)
XLA Modules:
  0.0 153.6 jit_solution(13361072166842339791)
XLA Ops:
  0.6 0.8 copy.19
  1.5 0.1 reshape.102
  1.6 0.3 fusion.11
  1.9 5.0 %convolution_add_fusion = f32[64,2048]{1,0:T(8,128)S(1)} fusion(bf16[64,2048]{1,0:T(8,128)(2,1)S(1)} %copy-done, bf16[2048,2048]{1,0:T(8,128)(2,1)} %param.12, bf16[64,2048]{1,0:T(8,128)(2,1)} %param.11), kind=kOutput, calls=%fused_computation.11 | convolution fusion | flops 537133056 | bytes 9437184 | tf_op jit(solution)/shard_map/dot_general | solution.py:31
  6.9 0.1 copy.20
  7.0 0.1 broadcast_in_dim.59
  7.1 0.2 select_reduce_fusion.1
  7.3 0.1 mul.72
  7.5 0.7 fusion.10
  8.2 0.1 multiply_reduce_fusion.1
  8.4 1.3 convert_bitcast_fusion.1
  9.7 64.2 %all_to_all.10 = bf16[128,8,2048]{2,1,0:T(8,128)(2,1)S(1)} all-to-all(bf16[128,8,2048]{2,1,0:T(8,128)(2,1)S(1)} %convert_bitcast_fusion.1), channel_id=1, replica_groups=mesh['dp'=16,'sub'=8] {'dp','sub'}, dimensions={0} | all-to-all | bytes 8388608 | tf_op jit(solution)/shard_map/all_to_all | solution.py:60
  74.0 8.9 %fusion = f32[1024,2048]{1,0:T(8,128)S(1)} fusion(bf16[1,2048,2048]{2,1,0:T(8,128)(2,1)S(1)} %copy-done.7, bf16[128,8,2048]{2,1,0:T(8,128)(2,1)S(1)} %all_to_all.10), kind=kOutput, calls=%fused_computation | convolution fusion | flops 8589934592 | bytes 20971520 | tf_op jit(solution)/shard_map/dot_general | solution.py:62
  82.9 1.4 fusion.2
  84.3 0.7 copy-done.8
  85.0 6.1 %convert_bitcast_fusion = bf16[128,8,2048]{2,1,0:T(8,128)(2,1)} fusion(bf16[1024,1024]{1,0:T(8,128)(2,1)S(1)} %fusion.2, bf16[1,1024,2048]{2,1,0:T(8,128)(2,1)S(1)} %copy-done.8), kind=kOutput, calls=%fused_computation.9 | convolution fusion | flops 4297064448 | bytes 10485760 | tf_op jit(solution)/shard_map/dot_general | solution.py:67
  91.1 5.6 %all-to-all-start.1 = ((bf16[128,8,2048]{2,1,0:T(8,128)(2,1)}), bf16[128,8,2048]{2,1,0:T(8,128)(2,1)}, u32[]{:S(2)}, u32[]{:S(2)}) async-start(bf16[128,8,2048]{2,1,0:T(8,128)(2,1)} %convert_bitcast_fusion), calls=%async_computation.1 | async-start | bytes 8388608 | tf_op jit(solution)/shard_map/all_to_all | solution.py:68
  96.8 0.3 fusion.28
  97.2 0.1 copy.21
  97.3 0.7 select_reduce_fusion
  98.0 51.5 %all-to-all-done.1 = bf16[128,8,2048]{2,1,0:T(8,128)(2,1)} async-done(((bf16[128,8,2048]{2,1,0:T(8,128)(2,1)}), bf16[128,8,2048]{2,1,0:T(8,128)(2,1)}, u32[]{:S(2)}, u32[]{:S(2)}) %all-to-all-start.1) | async-done | bytes 4194336 | tf_op jit(solution)/shard_map/all_to_all | solution.py:68
  149.5 2.9 %fusion.3 = f32[128,2048]{1,0:T(8,128)S(1)} fusion(bf16[128,8,2048]{2,1,0:T(8,128)(2,1)} %all-to-all-done.1, bf16[64,1024]{1,0:T(8,128)(2,1)S(1)} %get-tuple-element.5, bf16[64,1024]{1,0:T(8,128)(2,1)S(1)} %get-tuple-element.4), kind=kOutput, calls=%fused_computation.4 | convolution fusion | flops 537395200 | bytes 5505024 | tf_op jit(solution)/shard_map/dot_general | solution.py:76
  152.4 0.2 multiply_reduce_fusion
  152.6 0.9 multiply_multiply_fusion
  (28 shorter events, 0.3 us)
Async XLA Ops:
  0.6 1.2 copy-start
  1.9 5.0 %copy-start.6 = (s32[32,4]{0,1:T(4,128)S(1)}, s32[32,4]{0,1:T(4,128)}, u32[]{:S(2)}) copy-start(s32[32,4]{0,1:T(4,128)} %param.16) | copy-start | bytes 1540
  1.9 6.5 %copy-start.3 = (f32[2048]{0:T(1024)S(1)}, f32[2048]{0:T(1024)}, u32[]{:S(2)}) copy-start(f32[2048]{0:T(1024)} %param.13) | copy-start | bytes 24580
  9.7 64.2 %copy-start.7 = (bf16[1,2048,2048]{2,1,0:T(8,128)(2,1)S(1)}, bf16[1,2048,2048]{2,1,0:T(8,128)(2,1)}, u32[]{:S(2)}) copy-start(bf16[1,2048,2048]{2,1,0:T(8,128)(2,1)} %param.17) | copy-start | bytes 25165828
  82.9 2.2 %copy-start.8 = (bf16[1,1024,2048]{2,1,0:T(8,128)(2,1)S(1)}, bf16[1,1024,2048]{2,1,0:T(8,128)(2,1)}, u32[]{:S(2)}) copy-start(bf16[1,1024,2048]{2,1,0:T(8,128)(2,1)} %param.18) | copy-start | bytes 12582916
  91.1 5.7 %copy-start.2 = (bf16[2048,32]{0,1:T(8,128)(2,1)S(1)}, bf16[2048,32]{0,1:T(8,128)(2,1)}, u32[]{:S(2)}) copy-start(bf16[2048,32]{0,1:T(8,128)(2,1)} %param.14) | copy-start | bytes 393220
  91.1 6.0 %copy-start.4 = (s32[64,8]{0,1:T(8,128)S(1)}, s32[64,8]{0,1:T(8,128)}, u32[]{:S(2)}) copy-start(s32[64,8]{0,1:T(8,128)} %param.15) | copy-start | bytes 6148
  91.1 58.4 %all-to-all-start.1 = ((bf16[128,8,2048]{2,1,0:T(8,128)(2,1)}), bf16[128,8,2048]{2,1,0:T(8,128)(2,1)}, u32[]{:S(2)}, u32[]{:S(2)}) async-start(bf16[128,8,2048]{2,1,0:T(8,128)(2,1)} %convert_bitcast_fusion), calls=%async_computation.1 | async-start | bytes 8388608 | tf_op jit(solution)/shard_map/all_to_all | solution.py:68
  97.3 55.4 %copy-start.5 = (f32[2048]{0:T(1024)S(1)}, f32[2048]{0:T(1024)}, u32[]{:S(2)}) copy-start(f32[2048]{0:T(1024)} %param.19) | copy-start | bytes 24580
  152.6 1.0 copy-start.1

commit v7 on v2

--- a/solution.py
+++ b/solution.py
@@ -30,6 +30,7 @@
     slot_count = device_count * per_slot
     projected = jnp.dot(attn_heads, out_weight, preferred_element_type=jnp.float32)
     stream = residual.astype(jnp.float32) + projected
+    stream, expert_ids, holders = lax.optimization_barrier((stream, expert_ids, holders))
     normed = (stream * rms_factor(stream) * norm_gain).astype(jnp.bfloat16)
     logits = jnp.dot(normed, router_weight, preferred_element_type=jnp.float32)
     weights_all = jax.nn.softmax(logits, axis=-1)

time: 155 us -> 152 us (0.981)
  matrix products: 27.4 us -> 24.8 us
    dot_general x1, matrix products: 11.4 us -> 8.89 us  [body(): both_rows = jnp.dot(flat_rows, gate_up, preferred_element_type=jnp.float32)]
where the time goes in v7:
time: 152 us
  blocking collectives  64.2 us (42%)
  waiting for transfers between devices  51.5 us (34%)
  matrix products  24.8 us (16%)
  starting transfers between devices  5.64 us (4%)
  other arithmetic  3.1 us (2%)
  local copies, waits for them, and re-layouts  1.57 us (1%)
    all_to_all x1, blocking collectives, body(): lax.all_to_all(outgoing, ('dp', 'sub'), split_axis=0, concat_axis=0, tile...  64.2 us
    all_to_all x1, waiting for transfers between devices, body(): lax.all_to_all(answer.reshape(packet.shape), ('dp', 'sub'), split_axis=0,...  51.5 us
    dot_general x1, matrix products, body(): both_rows = jnp.dot(flat_rows, gate_up, preferred_element_type=jnp.float32)  8.89 us
    dot_general x1, matrix products, body(): jnp.dot(hidden, down_proj, preferred_element_type=jnp.float32)  6.14 us
    all_to_all x1, starting transfers between devices, body(): lax.all_to_all(answer.reshape(packet.shape), ('dp', 'sub'), split_axis=0,...  5.64 us
    dot_general x1, matrix products, body(): jnp.dot(attn_heads, out_weight, preferred_element_type=jnp.float32)  4.95 us
  transfers between devices with their start and end apart: 1, of which 1 were waited for; matrix products, arithmetic and copies ran while one was open for 1% of the time, Pallas kernels for 0%

profile of v7, /device:TPU:1, one launch (start us, length us, event | category | flops | bytes accessed | tf_op | source)
XLA Modules:
  0.0 151.6 jit_solution(18047559399619828252)
XLA Ops:
  0.7 0.9 copy-done
  1.6 5.0 %convolution_add_fusion = f32[64,2048]{1,0:T(8,128)S(1)} fusion(bf16[64,2048]{1,0:T(8,128)(2,1)S(1)} %copy-done, bf16[2048,2048]{1,0:T(8,128)(2,1)} %param.12, bf16[64,2048]{1,0:T(8,128)(2,1)} %param.11), kind=kOutput, calls=%fused_computation.11 | convolution fusion | flops 537133056 | bytes 9437184 | tf_op jit(solution)/shard_map/dot_general | solution.py:31
  6.6 0.1 copy.19
  6.6 0.1 reshape.102
  6.7 0.3 fusion.13
  7.1 0.1 copy.20
  7.1 0.1 broadcast_in_dim.59
  7.2 0.2 select_reduce_fusion.1
  7.5 0.1 mul.72
  7.6 0.1 convert_element_type.35
  7.7 0.7 fusion.12
  8.4 0.1 multiply_reduce_fusion.1
  8.6 1.3 convert_bitcast_fusion.1
  9.9 64.2 %all_to_all.10 = bf16[128,8,2048]{2,1,0:T(8,128)(2,1)S(1)} all-to-all(bf16[128,8,2048]{2,1,0:T(8,128)(2,1)S(1)} %convert_bitcast_fusion.1), channel_id=1, replica_groups=mesh['dp'=16,'sub'=8] {'dp','sub'}, dimensions={0} | all-to-all | bytes 8388608 | tf_op jit(solution)/shard_map/all_to_all | solution.py:60
  74.1 8.9 %fusion = f32[1024,2048]{1,0:T(8,128)S(1)} fusion(bf16[1,2048,2048]{2,1,0:T(8,128)(2,1)S(1)} %copy-done.7, bf16[128,8,2048]{2,1,0:T(8,128)(2,1)S(1)} %all_to_all.10), kind=kOutput, calls=%fused_computation | convolution fusion | flops 8589934592 | bytes 20971520 | tf_op jit(solution)/shard_map/dot_general | solution.py:62
  83.0 6.1 %convert_bitcast_fusion = bf16[128,8,2048]{2,1,0:T(8,128)(2,1)} fusion(bf16[1,1024,2048]{2,1,0:T(8,128)(2,1)S(1)} %copy-done.8, f32[1024,2048]{1,0:T(8,128)S(1)} %fusion), kind=kOutput, calls=%fused_computation.9 | convolution fusion | flops 4303355904 | bytes 16777216 | tf_op jit(solution)/shard_map/dot_general | solution.py:66
  89.2 5.6 %all-to-all-start.1 = ((bf16[128,8,2048]{2,1,0:T(8,128)(2,1)}), bf16[128,8,2048]{2,1,0:T(8,128)(2,1)}, u32[]{:S(2)}, u32[]{:S(2)}) async-start(bf16[128,8,2048]{2,1,0:T(8,128)(2,1)} %convert_bitcast_fusion), calls=%async_computation.1 | async-start | bytes 8388608 | tf_op jit(solution)/shard_map/all_to_all | solution.py:67
  94.8 0.3 fusion.31
  95.2 0.1 copy.21
  95.3 0.7 select_reduce_fusion
  96.1 51.5 %all-to-all-done.1 = bf16[128,8,2048]{2,1,0:T(8,128)(2,1)} async-done(((bf16[128,8,2048]{2,1,0:T(8,128)(2,1)}), bf16[128,8,2048]{2,1,0:T(8,128)(2,1)}, u32[]{:S(2)}, u32[]{:S(2)}) %all-to-all-start.1) | async-done | bytes 4194336 | tf_op jit(solution)/shard_map/all_to_all | solution.py:67
  147.6 2.9 %fusion.3 = f32[128,2048]{1,0:T(8,128)S(1)} fusion(bf16[128,8,2048]{2,1,0:T(8,128)(2,1)} %all-to-all-done.1, bf16[64,1024]{1,0:T(8,128)(2,1)S(1)} %get-tuple-element.11, bf16[64,1024]{1,0:T(8,128)(2,1)S(1)} %get-tuple-element.10), kind=kOutput, calls=%fused_computation.4 | convolution fusion | flops 537395200 | bytes 5505024 | tf_op jit(solution)/shard_map/dot_general | solution.py:75
  150.5 0.2 multiply_reduce_fusion
  150.7 0.9 multiply_multiply_fusion
  (27 shorter events, 0.2 us)
Async XLA Ops:
  0.6 1.0 copy-start
  0.6 5.9 %copy-start.4 = (s32[64,8]{0,1:T(8,128)S(1)}, s32[64,8]{0,1:T(8,128)}, u32[]{:S(2)}) copy-start(s32[64,8]{0,1:T(8,128)} %param.15) | copy-start | bytes 6148
  0.7 6.4 %copy-start.6 = (s32[32,4]{0,1:T(4,128)S(1)}, s32[32,4]{0,1:T(4,128)}, u32[]{:S(2)}) copy-start(s32[32,4]{0,1:T(4,128)} %param.16) | copy-start | bytes 1540
  0.7 7.9 %copy-start.3 = (f32[2048]{0:T(1024)S(1)}, f32[2048]{0:T(1024)}, u32[]{:S(2)}) copy-start(f32[2048]{0:T(1024)} %param.13) | copy-start | bytes 24580
  9.9 64.2 %copy-start.7 = (bf16[1,2048,2048]{2,1,0:T(8,128)(2,1)S(1)}, bf16[1,2048,2048]{2,1,0:T(8,128)(2,1)}, u32[]{:S(2)}) copy-start(bf16[1,2048,2048]{2,1,0:T(8,128)(2,1)} %param.17) | copy-start | bytes 25165828
  74.1 8.9 %copy-start.8 = (bf16[1,1024,2048]{2,1,0:T(8,128)(2,1)S(1)}, bf16[1,1024,2048]{2,1,0:T(8,128)(2,1)}, u32[]{:S(2)}) copy-start(bf16[1,1024,2048]{2,1,0:T(8,128)(2,1)} %param.18) | copy-start | bytes 12582916
  89.2 5.7 %copy-start.2 = (bf16[2048,32]{0,1:T(8,128)(2,1)S(1)}, bf16[2048,32]{0,1:T(8,128)(2,1)}, u32[]{:S(2)}) copy-start(bf16[2048,32]{0,1:T(8,128)(2,1)} %param.14) | copy-start | bytes 393220
  89.2 58.4 %all-to-all-start.1 = ((bf16[128,8,2048]{2,1,0:T(8,128)(2,1)}), bf16[128,8,2048]{2,1,0:T(8,128)(2,1)}, u32[]{:S(2)}, u32[]{:S(2)}) async-start(bf16[128,8,2048]{2,1,0:T(8,128)(2,1)} %convert_bitcast_fusion), calls=%async_computation.1 | async-start | bytes 8388608 | tf_op jit(solution)/shard_map/all_to_all | solution.py:67
  95.3 55.4 %copy-start.5 = (f32[2048]{0:T(1024)S(1)}, f32[2048]{0:T(1024)}, u32[]{:S(2)}) copy-start(f32[2048]{0:T(1024)} %param.19) | copy-start | bytes 24580
  150.7 1.0 copy-start.1

commit v8 on v5

--- a/solution.py
+++ b/solution.py
@@ -59,10 +59,9 @@
     down_proj = slot_down[0]
     packet = lax.all_to_all(outgoing, ("dp", "sub"), split_axis=0, concat_axis=0, tiled=True)
     flat_rows = packet.reshape(-1, model_width)
-    both_rows = jnp.dot(flat_rows, gate_up, preferred_element_type=jnp.float32)
-    hidden = (jax.nn.silu(both_rows[:, :hidden_width]) * both_rows[:, hidden_width:]).astype(
-        jnp.bfloat16
-    )
+    gate_rows = jnp.dot(flat_rows, gate_up[:, :hidden_width], preferred_element_type=jnp.float32)
+    up_rows = jnp.dot(flat_rows, gate_up[:, hidden_width:], preferred_element_type=jnp.float32)
+    hidden = (jax.nn.silu(gate_rows) * up_rows).astype(jnp.bfloat16)
     answer = jnp.dot(hidden, down_proj, preferred_element_type=jnp.float32).astype(jnp.bfloat16)
     returned = lax.all_to_all(
         answer.reshape(packet.shape), ("dp", "sub"), split_axis=0, concat_axis=0, tiled=True

time: 152 us -> 152 us (level)
    dot_general x1 -> x2, matrix products: 8.89 us -> 9.7 us  [the longest x1 5.2 us: body(): jnp.dot(flat_rows, gate_up[:, hidden_width:], preferred_element_type=jnp....]
where the time goes in v8:
time: 152 us
  blocking collectives  64.2 us (42%)
  waiting for transfers between devices  51.5 us (34%)
  matrix products  25.5 us (17%)
  starting transfers between devices  5.64 us (4%)
  other arithmetic  3.1 us (2%)
    all_to_all x1, blocking collectives, body(): lax.all_to_all(outgoing, ('dp', 'sub'), split_axis=0, concat_axis=0, tile...  64.2 us
    all_to_all x1, waiting for transfers between devices, body(): lax.all_to_all(answer.reshape(packet.shape), ('dp', 'sub'), split_axis=0,...  51.5 us
    dot_general x1, matrix products, body(): jnp.dot(hidden, down_proj, preferred_element_type=jnp.float32)  6.09 us
    all_to_all x1, starting transfers between devices, body(): lax.all_to_all(answer.reshape(packet.shape), ('dp', 'sub'), split_axis=0,...  5.64 us
    dot_general x1, matrix products, body(): jnp.dot(flat_rows, gate_up[:, hidden_width:], preferred_element_type=jnp....  5.2 us
    dot_general x1, matrix products, body(): jnp.dot(attn_heads, out_weight, preferred_element_type=jnp.float32)  4.96 us
    dot_general x1, matrix products, body(): jnp.dot(flat_rows, gate_up[:, :hidden_width], preferred_element_type=jnp....  4.49 us
  transfers between devices with their start and end apart: 1, of which 1 were waited for; matrix products, arithmetic and copies ran while one was open for 1% of the time, Pallas kernels for 0%

profile of v8, /device:TPU:1, one launch (start us, length us, event | category | flops | bytes accessed | tf_op | source)
XLA Modules:
  0.0 152.2 jit_solution(8056227242972180698)
XLA Ops:
  0.6 0.8 copy.19
  1.5 0.1 reshape.102
  1.6 0.3 fusion.17
  1.9 5.0 %convolution_add_fusion = f32[64,2048]{1,0:T(8,128)S(1)} fusion(bf16[64,2048]{1,0:T(8,128)(2,1)S(1)} %copy-done, bf16[2048,2048]{1,0:T(8,128)(2,1)} %param.12, bf16[64,2048]{1,0:T(8,128)(2,1)} %param.11), kind=kOutput, calls=%fused_computation.13 | convolution fusion | flops 537133056 | bytes 9437184 | tf_op jit(solution)/shard_map/dot_general | solution.py:31
  6.9 0.1 copy.20
  7.0 0.1 broadcast_in_dim.59
  7.1 0.2 select_reduce_fusion.1
  7.3 0.1 mul.72
  7.4 0.1 convert_element_type.35
  7.5 0.7 fusion.16
  8.2 0.1 multiply_reduce_fusion.1
  8.4 1.3 convert_bitcast_fusion.1
  9.7 64.2 %all_to_all.10 = bf16[128,8,2048]{2,1,0:T(8,128)(2,1)S(1)} all-to-all(bf16[128,8,2048]{2,1,0:T(8,128)(2,1)S(1)} %convert_bitcast_fusion.1), channel_id=1, replica_groups=mesh['dp'=16,'sub'=8] {'dp','sub'}, dimensions={0} | all-to-all | bytes 8388608 | tf_op jit(solution)/shard_map/all_to_all | solution.py:60
  74.0 4.5 %fusion.2 = f32[1024,1024]{1,0:T(8,128)S(1)} fusion(bf16[2048,2048]{1,0:T(8,128)(2,1)S(1)} %bitcast.28, bf16[128,8,2048]{2,1,0:T(8,128)(2,1)S(1)} %all_to_all.10), kind=kOutput, calls=%fused_computation.2 | convolution fusion | flops 4294967296 | bytes 12582912 | tf_op jit(solution)/shard_map/dot_general | solution.py:62
  78.5 5.2 %multiply_convert_fusion = bf16[1024,1024]{1,0:T(8,128)(2,1)S(1)} fusion(f32[1024,1024]{1,0:T(8,128)S(1)} %fusion.2, bf16[2048,2048]{1,0:T(8,128)(2,1)S(1)} %bitcast.29, bf16[128,8,2048]{2,1,0:T(8,128)(2,1)S(1)} %all_to_all.10), kind=kOutput, calls=%fused_computation.11 | convolution fusion | flops 4301258752 | bytes 14680064 | tf_op jit(solution)/shard_map/dot_general | solution.py:63
  83.7 6.1 %convert_bitcast_fusion = bf16[128,8,2048]{2,1,0:T(8,128)(2,1)} fusion(bf16[1024,1024]{1,0:T(8,128)(2,1)S(1)} %multiply_convert_fusion, bf16[1,1024,2048]{2,1,0:T(8,128)(2,1)S(1)} %copy-done.8), kind=kOutput, calls=%fused_computation.10 | convolution fusion | flops 4297064448 | bytes 10485760 | tf_op jit(solution)/shard_map/dot_general | solution.py:65
  89.8 5.6 %all-to-all-start.1 = ((bf16[128,8,2048]{2,1,0:T(8,128)(2,1)}), bf16[128,8,2048]{2,1,0:T(8,128)(2,1)}, u32[]{:S(2)}, u32[]{:S(2)}) async-start(bf16[128,8,2048]{2,1,0:T(8,128)(2,1)} %convert_bitcast_fusion), calls=%async_computation.1 | async-start | bytes 8388608 | tf_op jit(solution)/shard_map/all_to_all | solution.py:66
  95.4 0.3 fusion.34
  95.8 0.1 copy.21
  95.9 0.7 select_reduce_fusion
  96.7 51.5 %all-to-all-done.1 = bf16[128,8,2048]{2,1,0:T(8,128)(2,1)} async-done(((bf16[128,8,2048]{2,1,0:T(8,128)(2,1)}), bf16[128,8,2048]{2,1,0:T(8,128)(2,1)}, u32[]{:S(2)}, u32[]{:S(2)}) %all-to-all-start.1) | async-done | bytes 4194336 | tf_op jit(solution)/shard_map/all_to_all | solution.py:66
  148.1 2.9 %fusion.4 = f32[128,2048]{1,0:T(8,128)S(1)} fusion(bf16[128,8,2048]{2,1,0:T(8,128)(2,1)} %all-to-all-done.1, bf16[64,1024]{1,0:T(8,128)(2,1)S(1)} %get-tuple-element.5, bf16[64,1024]{1,0:T(8,128)(2,1)S(1)} %get-tuple-element.4), kind=kOutput, calls=%fused_computation.4 | convolution fusion | flops 537395200 | bytes 5505024 | tf_op jit(solution)/shard_map/dot_general | solution.py:74
  151.1 0.2 multiply_reduce_fusion
  151.3 0.9 multiply_multiply_fusion
  (28 shorter events, 0.2 us)
Async XLA Ops:
  0.6 1.2 copy-start
  1.9 5.0 %copy-start.6 = (s32[32,4]{0,1:T(4,128)S(1)}, s32[32,4]{0,1:T(4,128)}, u32[]{:S(2)}) copy-start(s32[32,4]{0,1:T(4,128)} %param.16) | copy-start | bytes 1540
  1.9 6.5 %copy-start.3 = (f32[2048]{0:T(1024)S(1)}, f32[2048]{0:T(1024)}, u32[]{:S(2)}) copy-start(f32[2048]{0:T(1024)} %param.13) | copy-start | bytes 24580
  9.7 64.2 %copy-start.7 = (bf16[1,2048,2048]{2,1,0:T(8,128)(2,1)S(1)}, bf16[1,2048,2048]{2,1,0:T(8,128)(2,1)}, u32[]{:S(2)}) copy-start(bf16[1,2048,2048]{2,1,0:T(8,128)(2,1)} %param.17) | copy-start | bytes 25165828
  78.5 5.2 %copy-start.8 = (bf16[1,1024,2048]{2,1,0:T(8,128)(2,1)S(1)}, bf16[1,1024,2048]{2,1,0:T(8,128)(2,1)}, u32[]{:S(2)}) copy-start(bf16[1,1024,2048]{2,1,0:T(8,128)(2,1)} %param.18) | copy-start | bytes 12582916
  89.8 5.6 %copy-start.2 = (bf16[2048,32]{0,1:T(8,128)(2,1)S(1)}, bf16[2048,32]{0,1:T(8,128)(2,1)}, u32[]{:S(2)}) copy-start(bf16[2048,32]{0,1:T(8,128)(2,1)} %param.14) | copy-start | bytes 393220
  89.8 6.0 %copy-start.4 = (s32[64,8]{0,1:T(8,128)S(1)}, s32[64,8]{0,1:T(8,128)}, u32[]{:S(2)}) copy-start(s32[64,8]{0,1:T(8,128)} %param.15) | copy-start | bytes 6148
  89.8 58.4 %all-to-all-start.1 = ((bf16[128,8,2048]{2,1,0:T(8,128)(2,1)}), bf16[128,8,2048]{2,1,0:T(8,128)(2,1)}, u32[]{:S(2)}, u32[]{:S(2)}) async-start(bf16[128,8,2048]{2,1,0:T(8,128)(2,1)} %convert_bitcast_fusion), calls=%async_computation.1 | async-start | bytes 8388608 | tf_op jit(solution)/shard_map/all_to_all | solution.py:66
  95.9 55.4 %copy-start.5 = (f32[2048]{0:T(1024)S(1)}, f32[2048]{0:T(1024)}, u32[]{:S(2)}) copy-start(f32[2048]{0:T(1024)} %param.19) | copy-start | bytes 24580
  151.3 1.0 copy-start.1

commit v9 on v5

--- a/solution.py
+++ b/solution.py
@@ -69,11 +69,7 @@
     )
     returned = returned.reshape(slot_count, model_width)
     mix = jnp.sum(jnp.where(hits, picked[None, :, :], 0.0), -1).T
-    mix_high = lax.reduce_precision(mix, exponent_bits=8, mantissa_bits=7)
-    mix_low = mix - mix_high
-    mix_both = jnp.concatenate([mix_high, mix_low], 0).astype(jnp.bfloat16)
-    summed = jnp.dot(mix_both, returned, preferred_element_type=jnp.float32)
-    expert_sum = summed[:tok_count] + summed[tok_count:]
+    expert_sum = jnp.dot(mix.astype(jnp.bfloat16), returned, preferred_element_type=jnp.float32)
     new_stream = stream + expert_sum
     next_normed = new_stream * rms_factor(new_stream) * next_gain
     return (new_stream, next_normed)

time: 152 us -> 155 us (1.020)
  matrix products: 24.8 us -> 27.5 us
    dot_general x1, matrix products: 8.89 us -> 11.4 us  [body(): both_rows = jnp.dot(flat_rows, gate_up, preferred_element_type=jnp.float32)]
where the time goes in v9:
time: 155 us
  blocking collectives  64.2 us (41%)
  waiting for transfers between devices  51.5 us (33%)
  matrix products  27.5 us (18%)
  starting transfers between devices  5.64 us (4%)
  other arithmetic  2.87 us (2%)
  local copies, waits for them, and re-layouts  2.06 us (1%)
    all_to_all x1, blocking collectives, body(): lax.all_to_all(outgoing, ('dp', 'sub'), split_axis=0, concat_axis=0, tile...  64.2 us
    all_to_all x1, waiting for transfers between devices, body(): lax.all_to_all(answer.reshape(packet.shape), ('dp', 'sub'), split_axis=0,...  51.5 us
    dot_general x1, matrix products, body(): both_rows = jnp.dot(flat_rows, gate_up, preferred_element_type=jnp.float32)  11.4 us
    dot_general x1, matrix products, body(): jnp.dot(hidden, down_proj, preferred_element_type=jnp.float32)  6.15 us
    all_to_all x1, starting transfers between devices, body(): lax.all_to_all(answer.reshape(packet.shape), ('dp', 'sub'), split_axis=0,...  5.64 us
    dot_general x1, matrix products, body(): jnp.dot(attn_heads, out_weight, preferred_element_type=jnp.float32)  4.96 us
    dot_general x1, matrix products, body(): jnp.dot(mix.astype(jnp.bfloat16), returned, preferred_element_type=jnp.fl...  3.15 us
  transfers between devices with their start and end apart: 1, of which 1 were waited for; matrix products, arithmetic and copies ran while one was open for 1% of the time, Pallas kernels for 0%

profile of v9, /device:TPU:1, one launch (start us, length us, event | category | flops | bytes accessed | tf_op | source)
XLA Modules:
  0.0 154.6 jit_solution(1704659608343927857)
XLA Ops:
  0.6 0.0 copy-start
  0.6 0.8 copy.19
  1.5 0.1 reshape.102
  1.6 0.3 fusion.16
  1.9 0.8 copy.20
  2.6 0.1 broadcast_in_dim.59
  2.7 0.2 select_reduce_fusion.1
  3.0 0.1 convert_element_type.38
  3.1 0.1 mul.72
  3.2 0.7 fusion.15
  3.9 5.0 %convolution_add_fusion = f32[64,2048]{1,0:T(8,128)S(1)} fusion(bf16[64,2048]{1,0:T(8,128)(2,1)S(1)} %copy-done, bf16[2048,2048]{1,0:T(8,128)(2,1)} %param.12, bf16[64,2048]{1,0:T(8,128)(2,1)} %param.11), kind=kOutput, calls=%fused_computation.12 | convolution fusion | flops 537133056 | bytes 9437184 | tf_op jit(solution)/shard_map/dot_general | solution.py:31
  8.9 0.1 multiply_reduce_fusion.1
  9.0 1.3 convert_bitcast_fusion.1
  10.4 64.2 %all_to_all.10 = bf16[128,8,2048]{2,1,0:T(8,128)(2,1)S(1)} all-to-all(bf16[128,8,2048]{2,1,0:T(8,128)(2,1)S(1)} %convert_bitcast_fusion.1), channel_id=1, replica_groups=mesh['dp'=16,'sub'=8] {'dp','sub'}, dimensions={0} | all-to-all | bytes 8388608 | tf_op jit(solution)/shard_map/all_to_all | solution.py:60
  74.6 11.4 %fusion = f32[1024,2048]{1,0:T(8,128)S(1)} fusion(bf16[1,2048,2048]{2,1,0:T(8,128)(2,1)} %param.17, bf16[128,8,2048]{2,1,0:T(8,128)(2,1)S(1)} %all_to_all.10), kind=kOutput, calls=%fused_computation | convolution fusion | flops 8589934592 | bytes 20971520 | tf_op jit(solution)/shard_map/dot_general | solution.py:62
  86.0 6.2 %convert_bitcast_fusion = bf16[128,8,2048]{2,1,0:T(8,128)(2,1)} fusion(bf16[1,1024,2048]{2,1,0:T(8,128)(2,1)S(1)} %copy-done.6, f32[1024,2048]{1,0:T(8,128)S(1)} %fusion), kind=kOutput, calls=%fused_computation.9 | convolution fusion | flops 4303355904 | bytes 16777216 | tf_op jit(solution)/shard_map/dot_general | solution.py:66
  92.1 5.6 %all-to-all-start.1 = ((bf16[128,8,2048]{2,1,0:T(8,128)(2,1)}), bf16[128,8,2048]{2,1,0:T(8,128)(2,1)}, u32[]{:S(2)}, u32[]{:S(2)}) async-start(bf16[128,8,2048]{2,1,0:T(8,128)(2,1)} %convert_bitcast_fusion), calls=%async_computation.1 | async-start | bytes 8388608 | tf_op jit(solution)/shard_map/all_to_all | solution.py:67
  97.8 0.3 fusion.28
  98.2 0.1 copy.21
  98.3 0.7 select_reduce_fusion
  99.0 51.5 %all-to-all-done.1 = bf16[128,8,2048]{2,1,0:T(8,128)(2,1)} async-done(((bf16[128,8,2048]{2,1,0:T(8,128)(2,1)}), bf16[128,8,2048]{2,1,0:T(8,128)(2,1)}, u32[]{:S(2)}, u32[]{:S(2)}) %all-to-all-start.1) | async-done | bytes 4194336 | tf_op jit(solution)/shard_map/all_to_all | solution.py:67
  150.5 3.1 %multiply_reduce_fusion = (f32[64]{0:T(128)S(1)}, f32[64,2048]{1,0:T(8,128)S(1)}) fusion(f32[64,2048]{1,0:T(8,128)S(1)} %convolution_add_fusion, bf16[1024,64]{0,1:T(8,128)(2,1)S(1)} %select_reduce_fusion, bf16[128,8,2048]{2,1,0:T(8,128)(2,1)} %all-to-all-done.1), kind=kOutput, calls=%fused_computation.21 | convolution fusion | flops 268828608 | bytes 5374208 | tf_op jit(solution)/shard_map/dot_general | solution.py:72
  153.7 0.0 copy-start.1
  153.7 0.9 multiply_multiply_fusion
  (21 shorter events, 0.2 us)
Async XLA Ops:
  0.6 3.3 %copy-start = (bf16[64,2048]{1,0:T(8,128)(2,1)S(1)}, bf16[64,2048]{1,0:T(8,128)(2,1)}, u32[]{:S(2)}) copy-start(bf16[64,2048]{1,0:T(8,128)(2,1)} %param.10) | copy-start | bytes 786436
  3.9 5.1 %copy-start.3 = (f32[2048]{0:T(1024)S(1)}, f32[2048]{0:T(1024)}, u32[]{:S(2)}) copy-start(f32[2048]{0:T(1024)} %param.13) | copy-start | bytes 24580
  74.6 11.4 %copy-start.6 = (bf16[1,1024,2048]{2,1,0:T(8,128)(2,1)S(1)}, bf16[1,1024,2048]{2,1,0:T(8,128)(2,1)}, u32[]{:S(2)}) copy-start(bf16[1,1024,2048]{2,1,0:T(8,128)(2,1)} %param.18) | copy-start | bytes 12582916
  92.1 5.7 %copy-start.2 = (bf16[2048,32]{0,1:T(8,128)(2,1)S(1)}, bf16[2048,32]{0,1:T(8,128)(2,1)}, u32[]{:S(2)}) copy-start(bf16[2048,32]{0,1:T(8,128)(2,1)} %param.14) | copy-start | bytes 393220
  92.1 6.0 %copy-start.4 = (s32[64,8]{0,1:T(8,128)S(1)}, s32[64,8]{0,1:T(8,128)}, u32[]{:S(2)}) copy-start(s32[64,8]{0,1:T(8,128)} %param.15) | copy-start | bytes 6148
  92.1 58.4 %all-to-all-start.1 = ((bf16[128,8,2048]{2,1,0:T(8,128)(2,1)}), bf16[128,8,2048]{2,1,0:T(8,128)(2,1)}, u32[]{:S(2)}, u32[]{:S(2)}) async-start(bf16[128,8,2048]{2,1,0:T(8,128)(2,1)} %convert_bitcast_fusion), calls=%async_computation.1 | async-start | bytes 8388608 | tf_op jit(solution)/shard_map/all_to_all | solution.py:67
  97.8 55.9 %copy-start.5 = (f32[2048]{0:T(1024)S(1)}, f32[2048]{0:T(1024)}, u32[]{:S(2)}) copy-start(f32[2048]{0:T(1024)} %param.19) | copy-start | bytes 24580
  153.7 1.0 copy-start.1
